TPU v7x, 128 devices: a whole 4x4x4 slice. The times are simulated.
128 devices in a mesh: node: 4 (over x), ep: 32 (over y, z, core).
Axes of the slice: x: 4, y: 4, z: 4, core: 2. Of those that a mesh axis runs over, the one named last changes fastest.
Arguments:
- images: bfloat16 [128, 257, 1280], P(('node', 'ep')), may hold values from -6 to 6
- w_query: bfloat16 [1280, 1280], P(None, 'node'), may hold values from -6 to 6
- w_key: bfloat16 [1280, 1280], P(None, 'node'), may hold values from -6 to 6
- w_value: bfloat16 [1280, 1280], P(None, 'node'), may hold values from -0.15625 to 0.15625
- w_output: bfloat16 [1280, 1280], replicated, may hold values from -0.15625 to 0.15625
- router: bfloat16 [1280, 32], replicated, may hold values from -0.15625 to 0.15625
- w_in: bfloat16 [32, 1280, 5120], P('ep', None, 'node'), may hold values from -0.15625 to 0.15625
- w_out: bfloat16 [32, 5120, 1280], P('ep', 'node'), may hold values from -0.078125 to 0.078125
- routes: int32 [128, 257, 2], P(('node', 'ep')), may hold values from 0 to 31, all different within a row; in each aligned block of 257 rows (0 to 256, 257 to 513, ..., all dimensions but the last counted through in order) at most 24 rows name the same one
Outputs:
- output: bfloat16 [128, 257, 1280], P(('node', 'ep'))
Inputs may be any that keep to these rules, and one draw needn't show every extreme that they name: `routes`: the two experts of a token differ. At most 24 tokens of one image name the same expert, and in every draw some image has an expert named by exactly 24 of its tokens.
All inputs are finite; a program needn't handle non-finite values.
Results may differ from a plain program's by a relative error of at most 0.0085.
Values may be sent and summed in bfloat16 or wider, within the bound.
No kernel may reach another device: no remote copies, remote signals or barrier semaphores. Data moves between devices by JAX's collectives and lax.ppermute only.
A program may use at most 128 MiB of HBM per device.

v0:
```python
import math

import jax
import jax.numpy as jnp
from jax import lax
from jax.sharding import PartitionSpec as P

D = 1280
HEADS = 16
CAP = 24


def layer_norm(values):
    center = values - jnp.mean(values, axis=-1, keepdims=True)
    spread = jnp.mean(center * center, axis=-1, keepdims=True)
    return center * lax.rsqrt(spread + 1e-06)


def slot_table(chosen, num_experts):
    onehot = (chosen[..., None] == jnp.arange(num_experts, dtype=jnp.int32)).astype(jnp.int32)
    before = jnp.cumsum(onehot, axis=1) - onehot
    return jnp.sum(before * onehot, axis=-1)


def shards(images, w_query, w_key, w_value, w_output, router, w_in, w_out, routes):
    local_images, tokens_dev, width = images.shape
    head_size = D // HEADS
    local_heads = w_query.shape[1] // head_size
    node_count = lax.axis_size("node")
    column_count = lax.axis_size("ep")
    num_experts = router.shape[1]
    local_experts = w_in.shape[0]
    slot_count = local_images * CAP
    inputs = images.astype(jnp.float32)
    normed = layer_norm(inputs).astype(jnp.bfloat16)
    shard_rows = lax.all_gather(normed, "node", axis=0, tiled=True)
    number = shard_rows.shape[0]
    queries = jnp.einsum(
        "ctd,de->cte", shard_rows, w_query, preferred_element_type=jnp.float32
    ).astype(jnp.bfloat16)
    projected_keys = jnp.einsum(
        "ctd,de->cte", shard_rows, w_key, preferred_element_type=jnp.float32
    ).astype(jnp.bfloat16)
    projected_values = jnp.einsum(
        "ctd,de->cte", shard_rows, w_value, preferred_element_type=jnp.float32
    ).astype(jnp.bfloat16)
    query_heads = queries.reshape(number, tokens_dev, local_heads, head_size)
    key_heads = projected_keys.reshape(number, tokens_dev, local_heads, head_size)
    value_heads = projected_values.reshape(number, tokens_dev, local_heads, head_size)
    scores = jnp.einsum(
        "cqhd,ckhd->chqk", query_heads, key_heads, preferred_element_type=jnp.float32
    ) / math.sqrt(head_size)
    weights = jax.nn.softmax(scores, axis=-1).astype(jnp.bfloat16)
    mixture = jnp.einsum(
        "chqk,ckhd->cqhd", weights, value_heads, preferred_element_type=jnp.float32
    ).astype(jnp.bfloat16)
    head_results = mixture.reshape(number, tokens_dev, local_heads * head_size)
    attention = jnp.einsum(
        "itd,de->ite",
        lax.all_to_all(head_results, "node", split_axis=0, concat_axis=2, tiled=True),
        w_output,
        preferred_element_type=jnp.float32,
    )
    middle = inputs + attention
    normed_second = layer_norm(middle).astype(jnp.bfloat16)
    logits = jnp.einsum("itd,de->ite", normed_second, router, preferred_element_type=jnp.float32)
    chosen_mask = routes[..., None] == jnp.arange(num_experts, dtype=jnp.int32)
    chosen_logit = jnp.sum(jnp.where(chosen_mask, logits[:, :, None, :], jnp.float32(0.0)), axis=-1)
    gate_values = jax.nn.sigmoid(chosen_logit)
    flat_routes = routes.reshape(local_images, 2 * tokens_dev)
    slot_index = slot_table(flat_routes, num_experts)
    image_base = jnp.arange(local_images, dtype=jnp.int32)[:, None] * CAP
    position = (flat_routes * slot_count + image_base + slot_index).reshape(-1)
    token_ids = jnp.arange(local_images * 2 * tokens_dev, dtype=jnp.int32) // 2
    source = jnp.full((num_experts * slot_count,), -1, jnp.int32).at[position].set(token_ids)
    token_rows = normed_second.reshape(local_images * tokens_dev, width)
    gathered = jnp.take(token_rows, jnp.maximum(source, 0), axis=0)
    gathered = jnp.where(source[:, None] >= 0, gathered, jnp.zeros_like(gathered))
    outgoing = gathered.reshape(column_count, local_experts, slot_count, width)
    copies = jnp.broadcast_to(outgoing[None], (node_count,) + outgoing.shape)
    copies = copies.reshape(node_count * column_count, local_experts, slot_count, width)
    arrived = lax.all_to_all(copies, ("node", "ep"), split_axis=0, concat_axis=0, tiled=True)
    pre_act = jnp.einsum("lesd,edf->lesf", arrived, w_in, preferred_element_type=jnp.float32)
    hidden = jax.nn.gelu(pre_act, approximate=True).astype(jnp.bfloat16)
    partial_sum = jnp.einsum(
        "lesf,efd->lesd", hidden, w_out, preferred_element_type=jnp.float32
    ).astype(jnp.bfloat16)
    returned = lax.all_to_all(partial_sum, ("node", "ep"), split_axis=0, concat_axis=0, tiled=True)
    returned = returned.astype(jnp.float32).reshape(
        node_count, column_count, local_experts, slot_count, width
    )
    expert_result = jnp.sum(returned, axis=0).astype(jnp.bfloat16)
    result_rows = expert_result.reshape(num_experts * slot_count, width)
    picked = jnp.take(result_rows, position, axis=0).reshape(local_images, tokens_dev, 2, width)
    expert_mix = jnp.sum(gate_values[..., None] * picked.astype(jnp.float32), axis=2)
    return (middle + expert_mix).astype(jnp.bfloat16)


def solution(mesh):
    placed = (
        P(("node", "ep"), None, None),
        P(None, "node"),
        P(None, "node"),
        P(None, "node"),
        P(),
        P(),
        P("ep", None, "node"),
        P("ep", "node", None),
        P(("node", "ep"), None, None),
    )
    return jax.shard_map(
        shards, mesh=mesh, in_specs=placed, out_specs=P(("node", "ep"), None, None), check_vma=False
    )
```

profile of v0, /device:TPU:1, one launch (start us, length us, event | category | flops | bytes accessed | tf_op | source)
XLA Modules:
  0.0 391.9 jit_solution(17544285698891339135)
XLA Ops:
  6.5 1.4 convert_reduce_fusion
  8.0 1.4 fusion.34
  9.4 2.3 fusion.35
  12.4 1.5 reduce-window.6
  15.9 4.1 %scatter_custom_fusion = s32[768]{0:T(1024)S(1)} fusion(s32[514]{0:T(1024)S(1)} %fusion.49, s32[514]{0:T(1024)S(1)} %add_select_fusion, s32[]{:T(128)} %constant.77.clone.1), kind=kCustom, calls=%fused_computation.80 | custom fusion | bytes 3076 | tf_op jit(solution)/shard_map/scatter | solution.py:75
  20.0 30.7 %all-gather.2.cloned.1.call-done = bf16[4,257,1280]{2,1,0:T(8,128)(2,1)} async-done(((bf16[1,257,1280]{2,1,0:T(8,128)(2,1)}), bf16[4,257,1280]{2,1,0:T(8,128)(2,1)}) %all-gather.2.cloned.1.call-update) | async-done | bytes 2631696 | tf_op jit(solution)/shard_map/all_gather | solution.py:36
  50.7 4.4 %convolution_convert_fusion = bf16[4,257,320]{2,1,0:T(8,128)(2,1)} fusion(bf16[4,257,1280]{2,1,0:T(8,128)(2,1)} %all-gather.2.cloned.1.call-done, bf16[1280,320]{0,1:T(8,128)(2,1)} %param.11), kind=kOutput, calls=%fused_computation.37 | convolution fusion | flops 842466560 | bytes 4108800 | tf_op jit(solution)/shard_map/ctd,de->cte/dot_general | solution.py:41
  55.1 2.3 copy.95
  57.4 4.4 %convolution_convert_fusion.2 = bf16[4,257,320]{2,1,0:T(8,128)(2,1)} fusion(bf16[4,257,1280]{2,1,0:T(8,128)(2,1)} %all-gather.2.cloned.1.call-done, bf16[1280,320]{0,1:T(8,128)(2,1)} %param.12), kind=kOutput, calls=%fused_computation.39 | convolution fusion | flops 842466560 | bytes 4108800 | tf_op jit(solution)/shard_map/ctd,de->cte/dot_general | solution.py:44
  61.9 2.2 copy.93
  64.1 4.4 %convolution_convert_fusion.1 = bf16[4,257,320]{2,1,0:T(8,128)(2,1)} fusion(bf16[4,257,1280]{2,1,0:T(8,128)(2,1)} %all-gather.2.cloned.1.call-done, bf16[1280,320]{0,1:T(8,128)(2,1)} %param.10), kind=kOutput, calls=%fused_computation.38 | convolution fusion | flops 842466560 | bytes 4108800 | tf_op jit(solution)/shard_map/ctd,de->cte/dot_general | solution.py:38
  68.5 2.3 copy.94
  70.8 6.5 %fusion.57 = (f32[4,4,257]{2,1,0:T(4,128)S(1)}, f32[4,4,257,257]{2,3,1,0:T(8,128)}) fusion(bf16[4,257,4,80]{1,3,2,0:T(8,128)(2,1)} %bitcast.114, bf16[4,257,4,80]{1,3,2,0:T(8,128)(2,1)} %bitcast.113), kind=kOutput, calls=%fused_computation.92 | convolution fusion | flops 172256048 | bytes 5559424 | tf_op jit(solution)/shard_map/sub | solution.py:53
  77.3 5.1 %fusion.33 = bf16[4,4,80,257]{3,2,1,0:T(8,128)(2,1)} fusion(bf16[4,257,4,80]{1,3,2,0:T(8,128)(2,1)} %bitcast.112, f32[4,4,257,257]{2,3,1,0:T(8,128)} %get-tuple-element.8, f32[4,4,257]{2,1,0:T(4,128)S(1)} %get-tuple-element.7), kind=kOutput, calls=%fused_computation.36 | convolution fusion | flops 171527968 | bytes 5559424 | tf_op jit(solution)/shard_map/chqk,ckhd->cqhd/dot_general | solution.py:54
  82.5 2.2 copy.97
  84.7 4.4 %all-to-all-start = ((bf16[4,257,320]{2,1,0:T(8,128)(2,1)}), bf16[4,257,320]{2,1,0:T(8,128)(2,1)}, u32[]{:S(2)}, u32[]{:S(2)}) async-start(bf16[4,257,320]{2,1,0:T(8,128)(2,1)} %copy.97), calls=%async_computation | async-start | bytes 1622016 | tf_op jit(solution)/shard_map/all_to_all | solution.py:60
  89.3 11.5 %all-to-all-done = bf16[4,257,320]{2,1,0:T(8,128)(2,1)} async-done(((bf16[4,257,320]{2,1,0:T(8,128)(2,1)}), bf16[4,257,320]{2,1,0:T(8,128)(2,1)}, u32[]{:S(2)}, u32[]{:S(2)}) %all-to-all-start) | async-done | bytes 657952 | tf_op jit(solution)/shard_map/all_to_all | solution.py:60
  100.8 2.3 copy.98
  103.1 2.5 reshape.358
  105.6 3.4 fusion.58
  110.2 1.1 fusion.40
  111.2 6.4 %gather_fusion = bf16[768,1280]{1,0:T(8,128)(2,1)} fusion(bf16[257,1280]{1,0:T(8,128)(2,1)} %fusion.40, s32[1024]{0:T(1024)S(1)} %pad_clamp_fusion.1), kind=kCustom, calls=%fused_computation | custom fusion | bytes 3935232 | tf_op jit(solution)/shard_map/jit(_take)/gather | solution.py:77
  117.6 1.9 select_select_fusion
  120.0 101.0 %all_to_all.25 = bf16[128,1,24,1280]{3,2,1,0:T(8,128)(2,1)} all-to-all(bf16[128,1,24,1280]{3,2,1,0:T(8,128)(2,1)S(1)} %bitcast.110), channel_id=1, replica_groups=mesh['node'=4,'ep'=32] {'node','ep'}, dimensions={0} | all-to-all | bytes 15728640 | tf_op jit(solution)/shard_map/all_to_all | solution.py:82
  221.0 25.9 %convert_bitcast_fusion = bf16[128,1,24,1280]{3,0,2,1:T(8,128)(2,1)} fusion(bf16[1,1280,1280]{2,1,0:T(8,128)(2,1)S(1)} %copy-done, bf16[128,1,24,1280]{3,2,1,0:T(8,128)(2,1)} %all_to_all.25, bf16[1,1280,1280]{2,1,0:T(8,128)(2,1)} %param.15), kind=kOutput, calls=%fused_computation.18 | convolution fusion | flops 20171980800 | bytes 22282240 | tf_op jit(solution)/shard_map/lesf,efd->lesd/dot_general | solution.py:85
  246.9 10.8 %copy.108 = bf16[128,1,24,1280]{3,2,1,0:T(8,128)(2,1)} copy(bf16[128,1,24,1280]{3,0,2,1:T(8,128)(2,1)} %convert_bitcast_fusion) | data formatting | bytes 15728640 | tf_op jit(solution)/shard_map/convert_element_type | solution.py:87
  257.6 8.2 %all-to-all-start.2 = ((bf16[128,1,24,1280]{3,2,1,0:T(8,128)(2,1)}), bf16[128,1,24,1280]{3,2,1,0:T(8,128)(2,1)}, u32[]{:S(2)}, u32[]{:S(2)}) async-start(bf16[128,1,24,1280]{3,2,1,0:T(8,128)(2,1)} %copy.108), calls=%async_computation.2 | async-start | bytes 15728640 | tf_op jit(solution)/shard_map/all_to_all | solution.py:88
  266.8 91.7 %all-to-all-done.2 = bf16[128,1,24,1280]{3,2,1,0:T(8,128)(2,1)} async-done(((bf16[128,1,24,1280]{3,2,1,0:T(8,128)(2,1)}), bf16[128,1,24,1280]{3,2,1,0:T(8,128)(2,1)}, u32[]{:S(2)}, u32[]{:S(2)}) %all-to-all-start.2) | async-done | bytes 7864352 | tf_op jit(solution)/shard_map/all_to_all | solution.py:88
  358.5 4.3 %bitcast_reduce_fusion = bf16[32,24,1280]{2,1,0:T(8,128)(2,1)S(1)} fusion(bf16[4,32,24,1280]{3,2,1,0:T(8,128)(2,1)} %bitcast.107), kind=kLoop, calls=%fused_computation.13 | loop fusion | flops 2949120 | bytes 9830400 | tf_op jit(solution)/shard_map/reduce_sum | solution.py:92
  362.8 3.5 gather_fusion.1
  366.3 4.1 %gather.15 = bf16[1,257,2,1280]{3,2,1,0:T(2,128)(2,1)} reshape(bf16[514,1280]{1,0:T(8,128)(2,1)} %gather_fusion.1) | data formatting | bytes 2631680 | tf_op jit(solution)/shard_map/jit(_take)/gather | solution.py:94
  370.4 13.6 %multiply_reduce_fusion.1 = f32[257,1280]{1,0:T(8,128)S(1)} fusion(bf16[1,257,2,1280]{3,2,1,0:T(2,128)(2,1)} %gather.15, pred[257,2]{1,0:T(8,128)(4,1)S(1)} %copy.105, f32[257,2]{1,0:T(8,128)S(1)} %copy.99), kind=kLoop, calls=%fused_computation.29 | loop fusion | flops 2302720 | bytes 2634250 | tf_op jit(solution)/shard_map/reduce_sum | solution.py:95
  (55 shorter events, 6.4 us)
Async XLA Ops:
  6.5 214.5 %copy-start = (bf16[1,1280,1280]{2,1,0:T(8,128)(2,1)S(1)}, bf16[1,1280,1280]{2,1,0:T(8,128)(2,1)}, u32[]{:S(2)}) copy-start(bf16[1,1280,1280]{2,1,0:T(8,128)(2,1)} %param.16) | copy-start | bytes 9830404
  6.5 5.2 %copy-start.6 = (s32[1,257,2]{1,2,0:T(2,128)S(1)}, s32[1,257,2]{1,2,0:T(2,128)}, u32[]{:S(2)}) copy-start(s32[1,257,2]{1,2,0:T(2,128)} %param.17) | copy-start | bytes 6172
  6.5 44.1 %all-gather.2.cloned.1.call-start = ((), (), s32[]{:S(2)}) async-start(), calls=%async_computation.3 | async-start | bytes 3379200 | tf_op jit(solution)/shard_map/all_gather | solution.py:36
  84.7 16.1 %all-to-all-start = ((bf16[4,257,320]{2,1,0:T(8,128)(2,1)}), bf16[4,257,320]{2,1,0:T(8,128)(2,1)}, u32[]{:S(2)}, u32[]{:S(2)}) async-start(bf16[4,257,320]{2,1,0:T(8,128)(2,1)} %copy.97), calls=%async_computation | async-start | bytes 1622016 | tf_op jit(solution)/shard_map/all_to_all | solution.py:60
  109.1 1.1 copy-start.3
  257.6 8.7 %copy-start.2 = (bf16[257,1280]{1,0:T(8,128)(2,1)S(1)}, bf16[257,1280]{1,0:T(8,128)(2,1)}, u32[]{:S(2)}) copy-start(bf16[257,1280]{1,0:T(8,128)(2,1)} %fusion.40) | copy-start | bytes 1973764
  257.6 8.7 %copy-start.5 = (bf16[1280,32]{0,1:T(8,128)(2,1)S(1)}, bf16[1280,32]{0,1:T(8,128)(2,1)}, u32[]{:S(2)}) copy-start(bf16[1280,32]{0,1:T(8,128)(2,1)} %param.14) | copy-start | bytes 245764
  257.6 100.9 %all-to-all-start.2 = ((bf16[128,1,24,1280]{3,2,1,0:T(8,128)(2,1)}), bf16[128,1,24,1280]{3,2,1,0:T(8,128)(2,1)}, u32[]{:S(2)}, u32[]{:S(2)}) async-start(bf16[128,1,24,1280]{3,2,1,0:T(8,128)(2,1)} %copy.108), calls=%async_computation.2 | async-start | bytes 15728640 | tf_op jit(solution)/shard_map/all_to_all | solution.py:88
  366.3 18.7 %copy-start.1 = (bf16[1,1280,1280]{2,1,0:T(8,128)(2,1)S(1)}, bf16[1,1280,1280]{2,1,0:T(8,128)(2,1)}, u32[]{:S(2)}) copy-start(bf16[1,1280,1280]{2,1,0:T(8,128)(2,1)} %param.16) | copy-start | bytes 9830404
  370.4 13.6 %copy-start.4 = (f32[1,257,1280]{2,1,0:T(8,128)S(1)}, f32[1,257,1280]{2,1,0:T(8,128)}, u32[]{:S(2)}) copy-start(f32[1,257,1280]{2,1,0:T(8,128)} %copy-done.3) | copy-start | bytes 3947524
Sparse Core Ops, SparseCore 0:
  11.8 38.7 all-gather.1
where the time goes:
time: 397 us; the launch traced here: 392 us
  waiting for transfers between devices  134 us (34%)
  blocking collectives  101 us (25%)
  matrix products  54.6 us (14%)
  local copies, waits for them, and re-layouts  46.4 us (12%)
  other arithmetic  29.8 us (8%)
  between operations  13.7 us (3%)
  starting transfers between devices  12.5 us (3%)
    all_to_all x1, blocking collectives, shards(): lax.all_to_all(copies, ('node', 'ep'), split_axis=0, concat_axis=0, tiled...  101 us
    all_to_all x1, waiting for transfers between devices, shards(): lax.all_to_all(partial_sum, ('node', 'ep'), split_axis=0, concat_axis=0,...  91.7 us
    all_gather x1, waiting for transfers between devices, shards(): shard_rows = lax.all_gather(normed, 'node', axis=0, tiled=True)  30.7 us
    dot_general x1, matrix products, shards(): jnp.einsum('lesf,efd->lesd', hidden, w_out, preferred_element_type=jnp.fl...  25.9 us
    reduce_sum x1, other arithmetic, shards(): jnp.sum(gate_values[..., None] * picked.astype(jnp.float32), axis=2)  13.6 us
    all_to_all x1, waiting for transfers between devices, shards(): lax.all_to_all(head_results, 'node', split_axis=0, concat_axis=2, tiled=T...  11.5 us
    convert_element_type x1, local copies, waits for them, and re-layouts, shards(): partial_sum = jnp.einsum('lesf,efd->lesd', hidden, w_out, preferred_eleme...  10.8 us
    all_to_all x1, starting transfers between devices, shards(): lax.all_to_all(partial_sum, ('node', 'ep'), split_axis=0, concat_axis=0,...  8.17 us
  transfers between devices with their start and end apart: 3, of which 3 were waited for; matrix products, arithmetic and copies ran while one was open for 2% of the time, Pallas kernels for 0%

commit v1 on v0

--- a/solution.py
+++ b/solution.py
@@ -77,19 +77,17 @@
     gathered = jnp.take(token_rows, jnp.maximum(source, 0), axis=0)
     gathered = jnp.where(source[:, None] >= 0, gathered, jnp.zeros_like(gathered))
     outgoing = gathered.reshape(column_count, local_experts, slot_count, width)
-    copies = jnp.broadcast_to(outgoing[None], (node_count,) + outgoing.shape)
-    copies = copies.reshape(node_count * column_count, local_experts, slot_count, width)
-    arrived = lax.all_to_all(copies, ("node", "ep"), split_axis=0, concat_axis=0, tiled=True)
+    by_column = lax.all_to_all(outgoing, "ep", split_axis=0, concat_axis=0, tiled=True)
+    arrived = lax.all_gather(by_column, "node", axis=0, tiled=True)
     pre_act = jnp.einsum("lesd,edf->lesf", arrived, w_in, preferred_element_type=jnp.float32)
     hidden = jax.nn.gelu(pre_act, approximate=True).astype(jnp.bfloat16)
     partial_sum = jnp.einsum(
         "lesf,efd->lesd", hidden, w_out, preferred_element_type=jnp.float32
     ).astype(jnp.bfloat16)
-    returned = lax.all_to_all(partial_sum, ("node", "ep"), split_axis=0, concat_axis=0, tiled=True)
-    returned = returned.astype(jnp.float32).reshape(
-        node_count, column_count, local_experts, slot_count, width
-    )
-    expert_result = jnp.sum(returned, axis=0).astype(jnp.bfloat16)
+    partial_sum = partial_sum.reshape(node_count * column_count * local_experts * slot_count, width)
+    summed = lax.psum_scatter(partial_sum, "node", scatter_dimension=0, tiled=True)
+    summed = summed.reshape(column_count, local_experts, slot_count, width)
+    expert_result = lax.all_to_all(summed, "ep", split_axis=0, concat_axis=0, tiled=True)
     result_rows = expert_result.reshape(num_experts * slot_count, width)
     picked = jnp.take(result_rows, position, axis=0).reshape(local_images, tokens_dev, 2, width)
     expert_mix = jnp.sum(gate_values[..., None] * picked.astype(jnp.float32), axis=2)

time: 397 us -> 411 us (1.035); the launches traced: 392 us -> 411 us
  waiting for transfers between devices: 134 us -> 220 us
  blocking collectives: 101 us -> 35.3 us
  other arithmetic: 29.8 us -> 25.5 us
    reduce_scatter x0 -> x1, waiting for transfers between devices: none -> 77.9 us  [shards(): lax.psum_scatter(partial_sum, 'node', scatter_dimension=0, tiled=True)]
    all_gather x0 -> x1, waiting for transfers between devices: none -> 74.3 us  [shards(): arrived = lax.all_gather(by_column, 'node', axis=0, tiled=True)]
    all_to_all x1, waiting for transfers between devices: 91.7 us -> 25.9 us  [shards(): lax.all_to_all(summed, 'ep', split_axis=0, concat_axis=0, tiled=True)]
    all_to_all x1, blocking collectives: 101 us -> 35.3 us  [shards(): lax.all_to_all(outgoing, 'ep', split_axis=0, concat_axis=0, tiled=True)]
    dot_general x0 -> x1, matrix products: none -> 15.5 us  [shards(): jnp.einsum('lesd,edf->lesf', arrived, w_in, preferred_element_type=jnp.fl...]
    dot_general x1, matrix products: 25.9 us -> 12.1 us  [shards(): jnp.einsum('lesf,efd->lesd', hidden, w_out, preferred_element_type=jnp.fl...]
    reduce_sum x1 -> x0, other arithmetic: 4.3 us -> none  [shards(): expert_result = jnp.sum(returned, axis=0).astype(jnp.bfloat16)]
  transfers between devices with their start and end apart: 3 -> 5, of which waited for: 3 -> 5; matrix products, arithmetic and copies ran while one was open for 2% -> 2% of each run, Pallas kernels for 0% -> 0%
where the time goes in v1:
time: 411 us
  waiting for transfers between devices  220 us (54%)
  matrix products  56.3 us (14%)
  local copies, waits for them, and re-layouts  47.6 us (12%)
  blocking collectives  35.3 us (9%)
  other arithmetic  25.5 us (6%)
  between operations  13.4 us (3%)
  starting transfers between devices  12.2 us (3%)
    reduce_scatter x1, waiting for transfers between devices, shards(): lax.psum_scatter(partial_sum, 'node', scatter_dimension=0, tiled=True)  77.9 us
    all_gather x1, waiting for transfers between devices, shards(): arrived = lax.all_gather(by_column, 'node', axis=0, tiled=True)  74.3 us
    all_to_all x1, blocking collectives, shards(): lax.all_to_all(outgoing, 'ep', split_axis=0, concat_axis=0, tiled=True)  35.3 us
    all_gather x1, waiting for transfers between devices, shards(): shard_rows = lax.all_gather(normed, 'node', axis=0, tiled=True)  30.7 us
    all_to_all x1, waiting for transfers between devices, shards(): lax.all_to_all(summed, 'ep', split_axis=0, concat_axis=0, tiled=True)  25.9 us
    dot_general x1, matrix products, shards(): jnp.einsum('lesd,edf->lesf', arrived, w_in, preferred_element_type=jnp.fl...  15.5 us
    reduce_sum x1, other arithmetic, shards(): jnp.sum(gate_values[..., None] * picked.astype(jnp.float32), axis=2)  13.6 us
    dot_general x1, matrix products, shards(): jnp.einsum('lesf,efd->lesd', hidden, w_out, preferred_element_type=jnp.fl...  12.1 us
  transfers between devices with their start and end apart: 5, of which 5 were waited for; matrix products, arithmetic and copies ran while one was open for 2% of the time, Pallas kernels for 0%

profile of v1, /device:TPU:1, one launch (start us, length us, event | category | flops | bytes accessed | tf_op | source)
XLA Modules:
  0.0 410.6 jit_solution(5979756977608437721)
XLA Ops:
  9.4 2.3 fusion.26
  12.4 1.5 reduce-window.6
  15.9 4.1 scatter_custom_fusion
  20.0 30.7 %all-gather.3.cloned.1.call-done = bf16[4,257,1280]{2,1,0:T(8,128)(2,1)} async-done(((bf16[1,257,1280]{2,1,0:T(8,128)(2,1)}), bf16[4,257,1280]{2,1,0:T(8,128)(2,1)}) %all-gather.3.cloned.1.call-update) | async-done | bytes 2631696 | tf_op jit(solution)/shard_map/all_gather | solution.py:36
  50.7 4.4 %convolution_convert_fusion = bf16[4,257,320]{2,1,0:T(8,128)(2,1)} fusion(bf16[4,257,1280]{2,1,0:T(8,128)(2,1)} %all-gather.3.cloned.1.call-done, bf16[1280,320]{0,1:T(8,128)(2,1)} %param.11), kind=kOutput, calls=%fused_computation.35 | convolution fusion | flops 842466560 | bytes 4108800 | tf_op jit(solution)/shard_map/ctd,de->cte/dot_general | solution.py:41
  55.1 2.3 copy.100
  57.4 4.4 %convolution_convert_fusion.2 = bf16[4,257,320]{2,1,0:T(8,128)(2,1)} fusion(bf16[4,257,1280]{2,1,0:T(8,128)(2,1)} %all-gather.3.cloned.1.call-done, bf16[1280,320]{0,1:T(8,128)(2,1)} %param.12), kind=kOutput, calls=%fused_computation.37 | convolution fusion | flops 842466560 | bytes 4108800 | tf_op jit(solution)/shard_map/ctd,de->cte/dot_general | solution.py:44
  61.9 2.2 copy.98
  64.1 4.4 %convolution_convert_fusion.1 = bf16[4,257,320]{2,1,0:T(8,128)(2,1)} fusion(bf16[4,257,1280]{2,1,0:T(8,128)(2,1)} %all-gather.3.cloned.1.call-done, bf16[1280,320]{0,1:T(8,128)(2,1)} %param.10), kind=kOutput, calls=%fused_computation.36 | convolution fusion | flops 842466560 | bytes 4108800 | tf_op jit(solution)/shard_map/ctd,de->cte/dot_general | solution.py:38
  68.5 2.3 copy.99
  70.8 6.5 %fusion.44 = (f32[4,4,257]{2,1,0:T(4,128)S(1)}, f32[4,4,257,257]{2,3,1,0:T(8,128)}) fusion(bf16[4,257,4,80]{1,3,2,0:T(8,128)(2,1)} %bitcast.105, bf16[4,257,4,80]{1,3,2,0:T(8,128)(2,1)} %bitcast.104), kind=kOutput, calls=%fused_computation.86 | convolution fusion | flops 172256048 | bytes 5559424 | tf_op jit(solution)/shard_map/sub | solution.py:53
  77.3 5.1 %fusion.24 = bf16[4,4,80,257]{3,2,1,0:T(8,128)(2,1)} fusion(bf16[4,257,4,80]{1,3,2,0:T(8,128)(2,1)} %bitcast.103, f32[4,4,257,257]{2,3,1,0:T(8,128)} %get-tuple-element.8, f32[4,4,257]{2,1,0:T(4,128)S(1)} %get-tuple-element.7), kind=kOutput, calls=%fused_computation.34 | convolution fusion | flops 171527968 | bytes 5559424 | tf_op jit(solution)/shard_map/chqk,ckhd->cqhd/dot_general | solution.py:54
  82.5 2.2 copy.102
  84.7 4.2 %all-to-all-start = ((bf16[4,257,320]{2,1,0:T(8,128)(2,1)}), bf16[4,257,320]{2,1,0:T(8,128)(2,1)}, u32[]{:S(2)}, u32[]{:S(2)}) async-start(bf16[4,257,320]{2,1,0:T(8,128)(2,1)} %copy.102), calls=%async_computation | async-start | bytes 1622016 | tf_op jit(solution)/shard_map/all_to_all | solution.py:60
  89.3 11.4 %all-to-all-done = bf16[4,257,320]{2,1,0:T(8,128)(2,1)} async-done(((bf16[4,257,320]{2,1,0:T(8,128)(2,1)}), bf16[4,257,320]{2,1,0:T(8,128)(2,1)}, u32[]{:S(2)}, u32[]{:S(2)}) %all-to-all-start) | async-done | bytes 657952 | tf_op jit(solution)/shard_map/all_to_all | solution.py:60
  100.8 2.3 copy.103
  103.1 2.5 reshape.356
  105.6 3.4 fusion.45
  111.2 6.4 %gather_fusion = bf16[768,1280]{1,0:T(8,128)(2,1)} fusion(bf16[257,1280]{1,0:T(8,128)(2,1)} %fusion.31, s32[1024]{0:T(1024)S(1)} %pad_clamp_fusion.1), kind=kCustom, calls=%fused_computation | custom fusion | bytes 3935232 | tf_op jit(solution)/shard_map/jit(_take)/gather | solution.py:77
  117.6 1.9 select_bitcast_fusion
  119.5 35.3 %all_to_all.25 = bf16[32,1,24,1280]{3,2,1,0:T(8,128)(2,1)S(1)} all-to-all(bf16[32,1,24,1280]{3,2,1,0:T(8,128)(2,1)S(1)} %select_bitcast_fusion), channel_id=1, replica_groups=mesh['node'=4,'ep'=32] {'ep'}, dimensions={0} | all-to-all | bytes 3932160 | tf_op jit(solution)/shard_map/all_to_all | solution.py:80
  154.8 1.8 copy.113
  156.6 74.3 %all-gather.5.cloned.1.call-done = bf16[128,1,24,1280]{3,0,2,1:T(8,128)(2,1)} async-done(((bf16[32,1,24,1280]{3,0,2,1:T(8,128)(2,1)}), bf16[128,1,24,1280]{3,0,2,1:T(8,128)(2,1)}) %all-gather.5.cloned.1.call-update) | async-done | bytes 7864336 | tf_op jit(solution)/shard_map/all_gather | solution.py:81
  230.8 15.5 %fusion.8 = bf16[128,1,24,1280]{3,0,2,1:T(8,128)(2,1)S(1)} fusion(bf16[128,1,24,1280]{3,0,2,1:T(8,128)(2,1)} %all-gather.5.cloned.1.call-done, bf16[1,1280,1280]{2,1,0:T(8,128)(2,1)S(1)} %copy-done), kind=kOutput, calls=%fused_computation.12 | convolution fusion | flops 10101719040 | bytes 19005440 | tf_op jit(solution)/shard_map/lesd,edf->lesf/dot_general | solution.py:82
  246.4 12.1 %convert_bitcast_fusion = bf16[128,1,24,1280]{3,0,2,1:T(8,128)(2,1)} fusion(bf16[128,1,24,1280]{3,0,2,1:T(8,128)(2,1)S(1)} %fusion.8, bf16[1,1280,1280]{2,1,0:T(8,128)(2,1)S(1)} %copy-done.7), kind=kOutput, calls=%fused_computation.16 | convolution fusion | flops 10070261760 | bytes 19005440 | tf_op jit(solution)/shard_map/lesf,efd->lesd/dot_general | solution.py:84
  258.5 10.7 %copy.114 = bf16[128,1,24,1280]{3,2,0,1:T(8,128)(2,1)} copy(bf16[128,1,24,1280]{3,0,2,1:T(8,128)(2,1)} %convert_bitcast_fusion) | data formatting | bytes 15728640 | tf_op jit(solution)/shard_map/convert_element_type | solution.py:86
  269.2 77.9 %reduce-scatter.2.cloned.1.call-done = bf16[768,1280]{1,0:T(8,128)(2,1)} async-done(((bf16[3072,1280]{1,0:T(8,128)(2,1)}), bf16[768,1280]{1,0:T(8,128)(2,1)}) %reduce-scatter.2.cloned.1.call-update) | async-done | bytes 1966096 | tf_op jit(solution)/shard_map/reduce_scatter | solution.py:88
  347.1 7.8 %all-to-all-start.2 = ((bf16[32,1,24,1280]{3,2,1,0:T(8,128)(2,1)}), bf16[32,1,24,1280]{3,2,1,0:T(8,128)(2,1)S(1)}, u32[]{:S(2)}, u32[]{:S(2)}) async-start(bf16[32,1,24,1280]{3,2,1,0:T(8,128)(2,1)} %bitcast.102), calls=%async_computation.3 | async-start | bytes 3932160 | tf_op jit(solution)/shard_map/all_to_all | solution.py:90
  356.0 25.9 %all-to-all-done.2 = bf16[32,1,24,1280]{3,2,1,0:T(8,128)(2,1)S(1)} async-done(((bf16[32,1,24,1280]{3,2,1,0:T(8,128)(2,1)}), bf16[32,1,24,1280]{3,2,1,0:T(8,128)(2,1)S(1)}, u32[]{:S(2)}, u32[]{:S(2)}) %all-to-all-start.2) | async-done | bytes 1966112 | tf_op jit(solution)/shard_map/all_to_all | solution.py:90
  381.9 3.4 gather_fusion.1
  385.3 4.1 %gather.15 = bf16[1,257,2,1280]{3,2,1,0:T(2,128)(2,1)} reshape(bf16[514,1280]{1,0:T(8,128)(2,1)} %gather_fusion.1) | data formatting | bytes 2631680 | tf_op jit(solution)/shard_map/jit(_take)/gather | solution.py:92
  389.5 13.6 %multiply_reduce_fusion.1 = f32[257,1280]{1,0:T(8,128)S(1)} fusion(bf16[1,257,2,1280]{3,2,1,0:T(2,128)(2,1)} %gather.15, pred[257,2]{1,0:T(8,128)(4,1)S(1)} %copy.110, f32[257,2]{1,0:T(8,128)S(1)} %copy.104), kind=kLoop, calls=%fused_computation.27 | loop fusion | flops 2302720 | bytes 2634250 | tf_op jit(solution)/shard_map/reduce_sum | solution.py:93
  (63 shorter events, 10.1 us)
Async XLA Ops:
  6.5 224.3 %copy-start = (bf16[1,1280,1280]{2,1,0:T(8,128)(2,1)S(1)}, bf16[1,1280,1280]{2,1,0:T(8,128)(2,1)}, u32[]{:S(2)}) copy-start(bf16[1,1280,1280]{2,1,0:T(8,128)(2,1)} %param.15) | copy-start | bytes 9830404
  6.5 5.2 %copy-start.6 = (s32[1,257,2]{1,2,0:T(2,128)S(1)}, s32[1,257,2]{1,2,0:T(2,128)}, u32[]{:S(2)}) copy-start(s32[1,257,2]{1,2,0:T(2,128)} %param.17) | copy-start | bytes 6172
  6.5 44.1 %all-gather.3.cloned.1.call-start = ((), (), s32[]{:S(2)}) async-start(), calls=%async_computation.4 | async-start | bytes 3379200 | tf_op jit(solution)/shard_map/all_gather | solution.py:36
  84.7 16.1 %all-to-all-start = ((bf16[4,257,320]{2,1,0:T(8,128)(2,1)}), bf16[4,257,320]{2,1,0:T(8,128)(2,1)}, u32[]{:S(2)}, u32[]{:S(2)}) async-start(bf16[4,257,320]{2,1,0:T(8,128)(2,1)} %copy.102), calls=%async_computation | async-start | bytes 1622016 | tf_op jit(solution)/shard_map/all_to_all | solution.py:60
  88.9 142.0 %all-gather.5.cloned.1.call-start = ((), (), s32[]{:S(2)}) async-start(), calls=%async_computation.5 | async-start | bytes 9830400 | tf_op jit(solution)/shard_map/all_gather | solution.py:81
  109.1 1.1 copy-start.3
  156.5 190.6 %reduce-scatter.2.cloned.1.call-start = ((), (), s32[]{:S(2)}) async-start(), calls=%async_computation.6 | async-start | bytes 9830400 | tf_op jit(solution)/shard_map/reduce_scatter | solution.py:88
  230.8 15.5 %copy-start.7 = (bf16[1,1280,1280]{2,1,0:T(8,128)(2,1)S(1)}, bf16[1,1280,1280]{2,1,0:T(8,128)(2,1)}, u32[]{:S(2)}) copy-start(bf16[1,1280,1280]{2,1,0:T(8,128)(2,1)} %param.16) | copy-start | bytes 9830404
  269.2 86.2 %copy-start.2 = (bf16[257,1280]{1,0:T(8,128)(2,1)S(1)}, bf16[257,1280]{1,0:T(8,128)(2,1)}, u32[]{:S(2)}) copy-start(bf16[257,1280]{1,0:T(8,128)(2,1)} %fusion.31) | copy-start | bytes 1973764
  269.2 86.2 %copy-start.5 = (bf16[1280,32]{0,1:T(8,128)(2,1)S(1)}, bf16[1280,32]{0,1:T(8,128)(2,1)}, u32[]{:S(2)}) copy-start(bf16[1280,32]{0,1:T(8,128)(2,1)} %param.14) | copy-start | bytes 245764
  347.1 34.7 %all-to-all-start.2 = ((bf16[32,1,24,1280]{3,2,1,0:T(8,128)(2,1)}), bf16[32,1,24,1280]{3,2,1,0:T(8,128)(2,1)S(1)}, u32[]{:S(2)}, u32[]{:S(2)}) async-start(bf16[32,1,24,1280]{3,2,1,0:T(8,128)(2,1)} %bitcast.102), calls=%async_computation.3 | async-start | bytes 3932160 | tf_op jit(solution)/shard_map/all_to_all | solution.py:90
  385.3 18.7 %copy-start.1 = (bf16[1,1280,1280]{2,1,0:T(8,128)(2,1)S(1)}, bf16[1,1280,1280]{2,1,0:T(8,128)(2,1)}, u32[]{:S(2)}) copy-start(bf16[1,1280,1280]{2,1,0:T(8,128)(2,1)} %param.15) | copy-start | bytes 9830404
  389.5 13.6 %copy-start.4 = (f32[1,257,1280]{2,1,0:T(8,128)S(1)}, f32[1,257,1280]{2,1,0:T(8,128)}, u32[]{:S(2)}) copy-start(f32[1,257,1280]{2,1,0:T(8,128)} %copy-done.3) | copy-start | bytes 3947524
Sparse Core Ops, SparseCore 0:
  11.8 38.7 all-gather.2
  156.7 74.1 all-gather.4
  269.3 77.7 reduce-scatter.1

commit v2 on v0

--- a/solution.py
+++ b/solution.py
@@ -80,11 +80,14 @@
     copies = jnp.broadcast_to(outgoing[None], (node_count,) + outgoing.shape)
     copies = copies.reshape(node_count * column_count, local_experts, slot_count, width)
     arrived = lax.all_to_all(copies, ("node", "ep"), split_axis=0, concat_axis=0, tiled=True)
-    pre_act = jnp.einsum("lesd,edf->lesf", arrived, w_in, preferred_element_type=jnp.float32)
+    rows = arrived.transpose(1, 0, 2, 3).reshape(local_experts, -1, width)
+    pre_act = jnp.einsum("esd,edf->esf", rows, w_in, preferred_element_type=jnp.float32)
     hidden = jax.nn.gelu(pre_act, approximate=True).astype(jnp.bfloat16)
     partial_sum = jnp.einsum(
-        "lesf,efd->lesd", hidden, w_out, preferred_element_type=jnp.float32
+        "esf,efd->esd", hidden, w_out, preferred_element_type=jnp.float32
     ).astype(jnp.bfloat16)
+    partial_sum = partial_sum.reshape(local_experts, node_count * column_count, slot_count, width)
+    partial_sum = partial_sum.transpose(1, 0, 2, 3)
     returned = lax.all_to_all(partial_sum, ("node", "ep"), split_axis=0, concat_axis=0, tiled=True)
     returned = returned.astype(jnp.float32).reshape(
         node_count, column_count, local_experts, slot_count, width

time: 397 us -> 386 us (0.972)
  local copies, waits for them, and re-layouts: 46.4 us -> 35.7 us
    convert_element_type x1 -> x0, local copies, waits for them, and re-layouts: 10.8 us -> none  [shards(): partial_sum = jnp.einsum('lesf,efd->lesd', hidden, w_out, preferred_eleme...]
where the time goes in v2:
time: 386 us; the launch traced here: 381 us
  waiting for transfers between devices  134 us (35%)
  blocking collectives  101 us (26%)
  matrix products  54.4 us (14%)
  local copies, waits for them, and re-layouts  35.7 us (9%)
  other arithmetic  29.8 us (8%)
  between operations  13.7 us (4%)
  starting transfers between devices  12.5 us (3%)
    all_to_all x1, blocking collectives, shards(): lax.all_to_all(copies, ('node', 'ep'), split_axis=0, concat_axis=0, tiled...  101 us
    all_to_all x1, waiting for transfers between devices, shards(): lax.all_to_all(partial_sum, ('node', 'ep'), split_axis=0, concat_axis=0,...  91.7 us
    all_gather x1, waiting for transfers between devices, shards(): shard_rows = lax.all_gather(normed, 'node', axis=0, tiled=True)  30.7 us
    dot_general x1, matrix products, shards(): jnp.einsum('esf,efd->esd', hidden, w_out, preferred_element_type=jnp.floa...  25.7 us
    reduce_sum x1, other arithmetic, shards(): jnp.sum(gate_values[..., None] * picked.astype(jnp.float32), axis=2)  13.6 us
    all_to_all x1, waiting for transfers between devices, shards(): lax.all_to_all(head_results, 'node', split_axis=0, concat_axis=2, tiled=T...  11.5 us
    all_to_all x1, starting transfers between devices, shards(): lax.all_to_all(partial_sum, ('node', 'ep'), split_axis=0, concat_axis=0,...  8.17 us
  transfers between devices with their start and end apart: 3, of which 3 were waited for; matrix products, arithmetic and copies ran while one was open for 2% of the time, Pallas kernels for 0%

profile of v2, /device:TPU:1, one launch (start us, length us, event | category | flops | bytes accessed | tf_op | source)
XLA Modules:
  0.0 380.9 jit_solution(7857259367008982327)
XLA Ops:
  6.5 1.4 convert_reduce_fusion
  8.0 1.4 fusion.30
  9.4 2.3 fusion.31
  12.4 1.5 reduce-window.6
  15.9 4.1 %scatter_custom_fusion = s32[768]{0:T(1024)S(1)} fusion(s32[514]{0:T(1024)S(1)} %fusion.45, s32[514]{0:T(1024)S(1)} %add_select_fusion, s32[]{:T(128)} %constant.77.clone.1), kind=kCustom, calls=%fused_computation.81 | custom fusion | bytes 3076 | tf_op jit(solution)/shard_map/scatter | solution.py:75
  20.0 30.7 %all-gather.2.cloned.1.call-done = bf16[4,257,1280]{2,1,0:T(8,128)(2,1)} async-done(((bf16[1,257,1280]{2,1,0:T(8,128)(2,1)}), bf16[4,257,1280]{2,1,0:T(8,128)(2,1)}) %all-gather.2.cloned.1.call-update) | async-done | bytes 2631696 | tf_op jit(solution)/shard_map/all_gather | solution.py:36
  50.7 4.4 %convolution_convert_fusion.1 = bf16[4,257,320]{2,1,0:T(8,128)(2,1)} fusion(bf16[4,257,1280]{2,1,0:T(8,128)(2,1)} %all-gather.2.cloned.1.call-done, bf16[1280,320]{0,1:T(8,128)(2,1)} %param.11), kind=kOutput, calls=%fused_computation.38 | convolution fusion | flops 842466560 | bytes 4108800 | tf_op jit(solution)/shard_map/ctd,de->cte/dot_general | solution.py:41
  55.1 2.3 copy.83
  57.4 4.4 %convolution_convert_fusion.3 = bf16[4,257,320]{2,1,0:T(8,128)(2,1)} fusion(bf16[4,257,1280]{2,1,0:T(8,128)(2,1)} %all-gather.2.cloned.1.call-done, bf16[1280,320]{0,1:T(8,128)(2,1)} %param.12), kind=kOutput, calls=%fused_computation.40 | convolution fusion | flops 842466560 | bytes 4108800 | tf_op jit(solution)/shard_map/ctd,de->cte/dot_general | solution.py:44
  61.9 2.2 copy.81
  64.1 4.4 %convolution_convert_fusion.2 = bf16[4,257,320]{2,1,0:T(8,128)(2,1)} fusion(bf16[4,257,1280]{2,1,0:T(8,128)(2,1)} %all-gather.2.cloned.1.call-done, bf16[1280,320]{0,1:T(8,128)(2,1)} %param.10), kind=kOutput, calls=%fused_computation.39 | convolution fusion | flops 842466560 | bytes 4108800 | tf_op jit(solution)/shard_map/ctd,de->cte/dot_general | solution.py:38
  68.5 2.3 copy.82
  70.8 6.5 %fusion.53 = (f32[4,4,257]{2,1,0:T(4,128)S(1)}, f32[4,4,257,257]{2,3,1,0:T(8,128)}) fusion(bf16[4,257,4,80]{1,3,2,0:T(8,128)(2,1)} %bitcast.91, bf16[4,257,4,80]{1,3,2,0:T(8,128)(2,1)} %bitcast.90), kind=kOutput, calls=%fused_computation.93 | convolution fusion | flops 172256048 | bytes 5559424 | tf_op jit(solution)/shard_map/sub | solution.py:53
  77.3 5.1 %fusion.29 = bf16[4,4,80,257]{3,2,1,0:T(8,128)(2,1)} fusion(bf16[4,257,4,80]{1,3,2,0:T(8,128)(2,1)} %bitcast.89, f32[4,4,257,257]{2,3,1,0:T(8,128)} %get-tuple-element.8, f32[4,4,257]{2,1,0:T(4,128)S(1)} %get-tuple-element.7), kind=kOutput, calls=%fused_computation.37 | convolution fusion | flops 171527968 | bytes 5559424 | tf_op jit(solution)/shard_map/chqk,ckhd->cqhd/dot_general | solution.py:54
  82.5 2.2 copy.85
  84.7 4.4 %all-to-all-start = ((bf16[4,257,320]{2,1,0:T(8,128)(2,1)}), bf16[4,257,320]{2,1,0:T(8,128)(2,1)}, u32[]{:S(2)}, u32[]{:S(2)}) async-start(bf16[4,257,320]{2,1,0:T(8,128)(2,1)} %copy.85), calls=%async_computation | async-start | bytes 1622016 | tf_op jit(solution)/shard_map/all_to_all | solution.py:60
  89.3 11.5 %all-to-all-done = bf16[4,257,320]{2,1,0:T(8,128)(2,1)} async-done(((bf16[4,257,320]{2,1,0:T(8,128)(2,1)}), bf16[4,257,320]{2,1,0:T(8,128)(2,1)}, u32[]{:S(2)}, u32[]{:S(2)}) %all-to-all-start) | async-done | bytes 657952 | tf_op jit(solution)/shard_map/all_to_all | solution.py:60
  100.8 2.3 copy.86
  103.1 2.5 reshape.369
  105.6 3.4 fusion.54
  110.2 1.1 fusion.36
  111.2 6.4 %gather_fusion = bf16[768,1280]{1,0:T(8,128)(2,1)} fusion(bf16[257,1280]{1,0:T(8,128)(2,1)} %fusion.36, s32[1024]{0:T(1024)S(1)} %pad_clamp_fusion.1), kind=kCustom, calls=%fused_computation | custom fusion | bytes 3935232 | tf_op jit(solution)/shard_map/jit(_take)/gather | solution.py:77
  117.6 1.9 select_select_fusion
  120.0 101.0 %all_to_all.25 = bf16[128,1,24,1280]{3,2,1,0:T(8,128)(2,1)} all-to-all(bf16[128,1,24,1280]{3,2,1,0:T(8,128)(2,1)S(1)} %bitcast.85), channel_id=1, replica_groups=mesh['node'=4,'ep'=32] {'node','ep'}, dimensions={0} | all-to-all | bytes 15728640 | tf_op jit(solution)/shard_map/all_to_all | solution.py:82
  221.0 25.7 %convolution_convert_fusion = bf16[3072,1280]{1,0:T(8,128)(2,1)} fusion(bf16[1,1280,1280]{2,1,0:T(8,128)(2,1)S(1)} %copy-done, bf16[3072,1280]{1,0:T(8,128)(2,1)} %bitcast.87, bf16[1,1280,1280]{2,1,0:T(8,128)(2,1)} %param.15), kind=kOutput, calls=%fused_computation.13 | convolution fusion | flops 20171980800 | bytes 22282240 | tf_op jit(solution)/shard_map/esf,efd->esd/dot_general | solution.py:86
  246.7 8.2 %all-to-all-start.2 = ((bf16[128,1,24,1280]{3,2,1,0:T(8,128)(2,1)}), bf16[128,1,24,1280]{3,2,1,0:T(8,128)(2,1)}, u32[]{:S(2)}, u32[]{:S(2)}) async-start(bf16[128,1,24,1280]{3,2,1,0:T(8,128)(2,1)} %bitcast.86), calls=%async_computation.2 | async-start | bytes 15728640 | tf_op jit(solution)/shard_map/all_to_all | solution.py:91
  255.9 91.7 %all-to-all-done.2 = bf16[128,1,24,1280]{3,2,1,0:T(8,128)(2,1)} async-done(((bf16[128,1,24,1280]{3,2,1,0:T(8,128)(2,1)}), bf16[128,1,24,1280]{3,2,1,0:T(8,128)(2,1)}, u32[]{:S(2)}, u32[]{:S(2)}) %all-to-all-start.2) | async-done | bytes 7864352 | tf_op jit(solution)/shard_map/all_to_all | solution.py:91
  347.6 4.3 %bitcast_reduce_fusion = bf16[32,24,1280]{2,1,0:T(8,128)(2,1)S(1)} fusion(bf16[4,32,24,1280]{3,2,1,0:T(8,128)(2,1)} %bitcast.82), kind=kLoop, calls=%fused_computation.14 | loop fusion | flops 2949120 | bytes 9830400 | tf_op jit(solution)/shard_map/reduce_sum | solution.py:95
  351.9 3.5 gather_fusion.1
  355.4 4.1 %gather.15 = bf16[1,257,2,1280]{3,2,1,0:T(2,128)(2,1)} reshape(bf16[514,1280]{1,0:T(8,128)(2,1)} %gather_fusion.1) | data formatting | bytes 2631680 | tf_op jit(solution)/shard_map/jit(_take)/gather | solution.py:97
  359.5 13.6 %multiply_reduce_fusion.1 = f32[257,1280]{1,0:T(8,128)S(1)} fusion(bf16[1,257,2,1280]{3,2,1,0:T(2,128)(2,1)} %gather.15, pred[257,2]{1,0:T(8,128)(4,1)S(1)} %copy.93, f32[257,2]{1,0:T(8,128)S(1)} %copy.87), kind=kLoop, calls=%fused_computation.30 | loop fusion | flops 2302720 | bytes 2634250 | tf_op jit(solution)/shard_map/reduce_sum | solution.py:98
  373.1 1.0 fusion.32
  (54 shorter events, 5.4 us)
Async XLA Ops:
  6.5 214.5 %copy-start = (bf16[1,1280,1280]{2,1,0:T(8,128)(2,1)S(1)}, bf16[1,1280,1280]{2,1,0:T(8,128)(2,1)}, u32[]{:S(2)}) copy-start(bf16[1,1280,1280]{2,1,0:T(8,128)(2,1)} %param.16) | copy-start | bytes 9830404
  6.5 5.2 %copy-start.6 = (s32[1,257,2]{1,2,0:T(2,128)S(1)}, s32[1,257,2]{1,2,0:T(2,128)}, u32[]{:S(2)}) copy-start(s32[1,257,2]{1,2,0:T(2,128)} %param.17) | copy-start | bytes 6172
  6.5 44.1 %all-gather.2.cloned.1.call-start = ((), (), s32[]{:S(2)}) async-start(), calls=%async_computation.3 | async-start | bytes 3379200 | tf_op jit(solution)/shard_map/all_gather | solution.py:36
  84.7 16.1 %all-to-all-start = ((bf16[4,257,320]{2,1,0:T(8,128)(2,1)}), bf16[4,257,320]{2,1,0:T(8,128)(2,1)}, u32[]{:S(2)}, u32[]{:S(2)}) async-start(bf16[4,257,320]{2,1,0:T(8,128)(2,1)} %copy.85), calls=%async_computation | async-start | bytes 1622016 | tf_op jit(solution)/shard_map/all_to_all | solution.py:60
  109.1 1.1 copy-start.3
  246.7 8.7 %copy-start.2 = (bf16[257,1280]{1,0:T(8,128)(2,1)S(1)}, bf16[257,1280]{1,0:T(8,128)(2,1)}, u32[]{:S(2)}) copy-start(bf16[257,1280]{1,0:T(8,128)(2,1)} %fusion.36) | copy-start | bytes 1973764
  246.7 8.7 %copy-start.5 = (bf16[1280,32]{0,1:T(8,128)(2,1)S(1)}, bf16[1280,32]{0,1:T(8,128)(2,1)}, u32[]{:S(2)}) copy-start(bf16[1280,32]{0,1:T(8,128)(2,1)} %param.14) | copy-start | bytes 245764
  246.7 100.9 %all-to-all-start.2 = ((bf16[128,1,24,1280]{3,2,1,0:T(8,128)(2,1)}), bf16[128,1,24,1280]{3,2,1,0:T(8,128)(2,1)}, u32[]{:S(2)}, u32[]{:S(2)}) async-start(bf16[128,1,24,1280]{3,2,1,0:T(8,128)(2,1)} %bitcast.86), calls=%async_computation.2 | async-start | bytes 15728640 | tf_op jit(solution)/shard_map/all_to_all | solution.py:91
  355.4 18.7 %copy-start.1 = (bf16[1,1280,1280]{2,1,0:T(8,128)(2,1)S(1)}, bf16[1,1280,1280]{2,1,0:T(8,128)(2,1)}, u32[]{:S(2)}) copy-start(bf16[1,1280,1280]{2,1,0:T(8,128)(2,1)} %param.16) | copy-start | bytes 9830404
  359.5 13.6 %copy-start.4 = (f32[1,257,1280]{2,1,0:T(8,128)S(1)}, f32[1,257,1280]{2,1,0:T(8,128)}, u32[]{:S(2)}) copy-start(f32[1,257,1280]{2,1,0:T(8,128)} %copy-done.3) | copy-start | bytes 3947524
Sparse Core Ops, SparseCore 0:
  11.8 38.7 all-gather.1

commit v3 on v2

--- a/solution.py
+++ b/solution.py
@@ -71,11 +71,14 @@
     slot_index = slot_table(flat_routes, num_experts)
     image_base = jnp.arange(local_images, dtype=jnp.int32)[:, None] * CAP
     position = (flat_routes * slot_count + image_base + slot_index).reshape(-1)
-    token_ids = jnp.arange(local_images * 2 * tokens_dev, dtype=jnp.int32) // 2
-    source = jnp.full((num_experts * slot_count,), -1, jnp.int32).at[position].set(token_ids)
-    token_rows = normed_second.reshape(local_images * tokens_dev, width)
-    gathered = jnp.take(token_rows, jnp.maximum(source, 0), axis=0)
-    gathered = jnp.where(source[:, None] >= 0, gathered, jnp.zeros_like(gathered))
+    token_count = local_images * tokens_dev
+    token_slots = position.reshape(token_count, 2)
+    slot_ids = jnp.arange(num_experts * slot_count, dtype=jnp.int32)
+    token_rows = normed_second.reshape(token_count, width)
+    hits = (token_slots[None, :, 0] == slot_ids[:, None]) | (token_slots[None, :, 1] == slot_ids[:, None])
+    gathered = jnp.dot(
+        hits.astype(jnp.bfloat16), token_rows, preferred_element_type=jnp.float32
+    ).astype(jnp.bfloat16)
     outgoing = gathered.reshape(column_count, local_experts, slot_count, width)
     copies = jnp.broadcast_to(outgoing[None], (node_count,) + outgoing.shape)
     copies = copies.reshape(node_count * column_count, local_experts, slot_count, width)
@@ -94,8 +97,14 @@
     )
     expert_result = jnp.sum(returned, axis=0).astype(jnp.bfloat16)
     result_rows = expert_result.reshape(num_experts * slot_count, width)
-    picked = jnp.take(result_rows, position, axis=0).reshape(local_images, tokens_dev, 2, width)
-    expert_mix = jnp.sum(gate_values[..., None] * picked.astype(jnp.float32), axis=2)
+    flat_gates = gate_values.reshape(token_count, 2)
+    combine = jnp.where(token_slots[:, 0:1] == slot_ids[None, :], flat_gates[:, 0:1], jnp.float32(0.0)) + jnp.where(
+        token_slots[:, 1:2] == slot_ids[None, :], flat_gates[:, 1:2], jnp.float32(0.0)
+    )
+    expert_mix = jnp.dot(
+        combine, result_rows.astype(jnp.float32), precision=lax.Precision.HIGHEST,
+        preferred_element_type=jnp.float32,
+    ).reshape(local_images, tokens_dev, width)
     return (middle + expert_mix).astype(jnp.bfloat16)
 
 

time: 386 us -> 359 us (0.930)
  local copies, waits for them, and re-layouts: 35.7 us -> 19.3 us
  other arithmetic: 29.8 us -> 14.1 us
  matrix products: 54.4 us -> 58.6 us
    gather x3 -> x0, local copies, waits for them, and re-layouts: 14 us -> none  [the longest x2 7.59 us: shards(): jnp.take(result_rows, position, axis=0)]
    reduce_sum x1 -> x0, other arithmetic: 13.6 us -> none  [shards(): jnp.sum(gate_values[..., None] * picked.astype(jnp.float32), axis=2)]
    dot_general x0 -> x2, matrix products: none -> 4.17 us  [the longest x1 2.93 us: shards(): jnp.dot(combine, result_rows.astype(jnp.float32), precision=lax.Precision...]
    scatter x1 -> x0, local copies, waits for them, and re-layouts: 4.1 us -> none  [shards(): jnp.full((num_experts * slot_count,), -1, jnp.int32).at[position]]
where the time goes in v3:
time: 359 us; the launch traced here: 354 us
  waiting for transfers between devices  135 us (38%)
  blocking collectives  101 us (28%)
  matrix products  58.6 us (16%)
  local copies, waits for them, and re-layouts  19.3 us (5%)
  other arithmetic  14.1 us (4%)
  between operations  13.6 us (4%)
  starting transfers between devices  12.5 us (3%)
    all_to_all x1, blocking collectives, shards(): lax.all_to_all(copies, ('node', 'ep'), split_axis=0, concat_axis=0, tiled...  101 us
    all_to_all x1, waiting for transfers between devices, shards(): lax.all_to_all(partial_sum, ('node', 'ep'), split_axis=0, concat_axis=0,...  92.2 us
    all_gather x1, waiting for transfers between devices, shards(): shard_rows = lax.all_gather(normed, 'node', axis=0, tiled=True)  32.3 us
    dot_general x1, matrix products, shards(): jnp.einsum('esf,efd->esd', hidden, w_out, preferred_element_type=jnp.floa...  25.7 us
    all_to_all x1, waiting for transfers between devices, shards(): lax.all_to_all(head_results, 'node', split_axis=0, concat_axis=2, tiled=T...  10.4 us
    all_to_all x1, starting transfers between devices, shards(): lax.all_to_all(partial_sum, ('node', 'ep'), split_axis=0, concat_axis=0,...  8.17 us
  transfers between devices with their start and end apart: 3, of which 3 were waited for; matrix products, arithmetic and copies ran while one was open for 2% of the time, Pallas kernels for 0%

profile of v3, /device:TPU:1, one launch (start us, length us, event | category | flops | bytes accessed | tf_op | source)
XLA Modules:
  0.0 354.0 jit_solution(10390673403190029145)
XLA Ops:
  6.5 1.4 convert_reduce_fusion
  8.0 1.4 fusion.32
  9.4 2.3 fusion.33
  12.0 0.6 copy_bitcast_fusion
  12.7 3.0 reduce-window.6
  16.0 0.8 broadcast.148
  16.8 1.6 reshape.283
  18.4 32.3 %all-gather.2.cloned.1.call-done = bf16[4,257,1280]{2,1,0:T(8,128)(2,1)} async-done(((bf16[1,257,1280]{2,1,0:T(8,128)(2,1)}), bf16[4,257,1280]{2,1,0:T(8,128)(2,1)}) %all-gather.2.cloned.1.call-update) | async-done | bytes 2631696 | tf_op jit(solution)/shard_map/all_gather | solution.py:36
  50.7 4.4 %convolution_convert_fusion.2 = bf16[4,257,320]{2,1,0:T(8,128)(2,1)} fusion(bf16[4,257,1280]{2,1,0:T(8,128)(2,1)} %all-gather.2.cloned.1.call-done, bf16[1280,320]{0,1:T(8,128)(2,1)} %param.11), kind=kOutput, calls=%fused_computation.36 | convolution fusion | flops 842466560 | bytes 4108800 | tf_op jit(solution)/shard_map/ctd,de->cte/dot_general | solution.py:41
  55.1 2.3 copy.63
  57.4 4.4 %convolution_convert_fusion.4 = bf16[4,257,320]{2,1,0:T(8,128)(2,1)} fusion(bf16[4,257,1280]{2,1,0:T(8,128)(2,1)} %all-gather.2.cloned.1.call-done, bf16[1280,320]{0,1:T(8,128)(2,1)} %param.12), kind=kOutput, calls=%fused_computation.38 | convolution fusion | flops 842466560 | bytes 4108800 | tf_op jit(solution)/shard_map/ctd,de->cte/dot_general | solution.py:44
  61.9 2.2 copy.61
  64.1 4.4 %convolution_convert_fusion.3 = bf16[4,257,320]{2,1,0:T(8,128)(2,1)} fusion(bf16[4,257,1280]{2,1,0:T(8,128)(2,1)} %all-gather.2.cloned.1.call-done, bf16[1280,320]{0,1:T(8,128)(2,1)} %param.10), kind=kOutput, calls=%fused_computation.37 | convolution fusion | flops 842466560 | bytes 4108800 | tf_op jit(solution)/shard_map/ctd,de->cte/dot_general | solution.py:38
  68.5 2.3 copy.62
  70.8 6.5 %fusion.61 = (f32[4,4,257]{2,1,0:T(4,128)S(1)}, f32[4,4,257,257]{2,3,1,0:T(8,128)}) fusion(bf16[4,257,4,80]{1,3,2,0:T(8,128)(2,1)} %bitcast.95, bf16[4,257,4,80]{1,3,2,0:T(8,128)(2,1)} %bitcast.94), kind=kOutput, calls=%fused_computation.91 | convolution fusion | flops 172256048 | bytes 5559424 | tf_op jit(solution)/shard_map/sub | solution.py:53
  77.3 5.1 %fusion.31 = bf16[4,4,80,257]{3,2,1,0:T(8,128)(2,1)} fusion(bf16[4,257,4,80]{1,3,2,0:T(8,128)(2,1)} %bitcast.93, f32[4,4,257,257]{2,3,1,0:T(8,128)} %get-tuple-element.10, f32[4,4,257]{2,1,0:T(4,128)S(1)} %get-tuple-element.9), kind=kOutput, calls=%fused_computation.35 | convolution fusion | flops 171527968 | bytes 5559424 | tf_op jit(solution)/shard_map/chqk,ckhd->cqhd/dot_general | solution.py:54
  82.5 2.2 copy.65
  84.7 4.4 %all-to-all-start = ((bf16[4,257,320]{2,1,0:T(8,128)(2,1)}), bf16[4,257,320]{2,1,0:T(8,128)(2,1)}, u32[]{:S(2)}, u32[]{:S(2)}) async-start(bf16[4,257,320]{2,1,0:T(8,128)(2,1)} %copy.65), calls=%async_computation | async-start | bytes 1622016 | tf_op jit(solution)/shard_map/all_to_all | solution.py:60
  89.1 0.9 fusion.54
  90.4 10.4 %all-to-all-done = bf16[4,257,320]{2,1,0:T(8,128)(2,1)} async-done(((bf16[4,257,320]{2,1,0:T(8,128)(2,1)}), bf16[4,257,320]{2,1,0:T(8,128)(2,1)}, u32[]{:S(2)}, u32[]{:S(2)}) %all-to-all-start) | async-done | bytes 657952 | tf_op jit(solution)/shard_map/all_to_all | solution.py:60
  100.8 2.3 copy.66
  103.1 2.5 reshape.277
  105.6 3.4 fusion.62
  109.4 0.7 copy-done.2
  110.4 1.2 convolution_convert_fusion.1
  111.6 0.5 broadcast_in_dim.65
  112.2 101.0 %all_to_all.25 = bf16[128,1,24,1280]{3,2,1,0:T(8,128)(2,1)} all-to-all(bf16[128,1,24,1280]{3,2,1,0:T(8,128)(2,1)S(1)} %bitcast.87), channel_id=1, replica_groups=mesh['node'=4,'ep'=32] {'node','ep'}, dimensions={0} | all-to-all | bytes 15728640 | tf_op jit(solution)/shard_map/all_to_all | solution.py:85
  213.2 25.7 %convolution_convert_fusion = bf16[3072,1280]{1,0:T(8,128)(2,1)} fusion(bf16[1,1280,1280]{2,1,0:T(8,128)(2,1)S(1)} %copy-done, bf16[3072,1280]{1,0:T(8,128)(2,1)} %bitcast.89, bf16[1,1280,1280]{2,1,0:T(8,128)(2,1)} %param.15), kind=kOutput, calls=%fused_computation.10 | convolution fusion | flops 20171980800 | bytes 22282240 | tf_op jit(solution)/shard_map/esf,efd->esd/dot_general | solution.py:89
  238.8 8.2 %all-to-all-start.2 = ((bf16[128,1,24,1280]{3,2,1,0:T(8,128)(2,1)}), bf16[128,1,24,1280]{3,2,1,0:T(8,128)(2,1)}, u32[]{:S(2)}, u32[]{:S(2)}) async-start(bf16[128,1,24,1280]{3,2,1,0:T(8,128)(2,1)} %bitcast.88), calls=%async_computation.2 | async-start | bytes 15728640 | tf_op jit(solution)/shard_map/all_to_all | solution.py:94
  247.6 92.2 %all-to-all-done.2 = bf16[128,1,24,1280]{3,2,1,0:T(8,128)(2,1)} async-done(((bf16[128,1,24,1280]{3,2,1,0:T(8,128)(2,1)}), bf16[128,1,24,1280]{3,2,1,0:T(8,128)(2,1)}, u32[]{:S(2)}, u32[]{:S(2)}) %all-to-all-start.2) | async-done | bytes 7864352 | tf_op jit(solution)/shard_map/all_to_all | solution.py:94
  339.8 4.4 %bitcast_reduce_fusion = bf16[32,24,1280]{2,1,0:T(8,128)(2,1)S(1)} fusion(bf16[4,32,24,1280]{3,2,1,0:T(8,128)(2,1)} %bitcast.86), kind=kLoop, calls=%fused_computation.11 | loop fusion | flops 2949120 | bytes 9830400 | tf_op jit(solution)/shard_map/reduce_sum | solution.py:98
  344.2 2.9 fusion.28
  (40 shorter events, 2.2 us)
Async XLA Ops:
  6.5 206.6 %copy-start = (bf16[1,1280,1280]{2,1,0:T(8,128)(2,1)S(1)}, bf16[1,1280,1280]{2,1,0:T(8,128)(2,1)}, u32[]{:S(2)}) copy-start(bf16[1,1280,1280]{2,1,0:T(8,128)(2,1)} %param.16) | copy-start | bytes 9830404
  6.5 5.2 %copy-start.7 = (s32[1,257,2]{1,2,0:T(2,128)S(1)}, s32[1,257,2]{1,2,0:T(2,128)}, u32[]{:S(2)}) copy-start(s32[1,257,2]{1,2,0:T(2,128)} %param.17) | copy-start | bytes 6172
  6.5 44.1 %all-gather.2.cloned.1.call-start = ((), (), s32[]{:S(2)}) async-start(), calls=%async_computation.3 | async-start | bytes 3379200 | tf_op jit(solution)/shard_map/all_gather | solution.py:36
  84.7 16.1 %all-to-all-start = ((bf16[4,257,320]{2,1,0:T(8,128)(2,1)}), bf16[4,257,320]{2,1,0:T(8,128)(2,1)}, u32[]{:S(2)}, u32[]{:S(2)}) async-start(bf16[4,257,320]{2,1,0:T(8,128)(2,1)} %copy.65), calls=%async_computation | async-start | bytes 1622016 | tf_op jit(solution)/shard_map/all_to_all | solution.py:60
  109.1 1.1 copy-start.2
  110.4 1.3 copy-start.4
  238.8 8.3 %copy-start.5 = (bf16[257,1280]{1,0:T(8,128)(2,1)S(1)}, bf16[257,1280]{1,0:T(8,128)(2,1)}, u32[]{:S(2)}) copy-start(bf16[257,1280]{1,0:T(8,128)(2,1)} %copy-done.4) | copy-start | bytes 1973764
  238.8 8.3 %copy-start.6 = (bf16[1280,32]{0,1:T(8,128)(2,1)S(1)}, bf16[1280,32]{0,1:T(8,128)(2,1)}, u32[]{:S(2)}) copy-start(bf16[1280,32]{0,1:T(8,128)(2,1)} %param.14) | copy-start | bytes 245764
  238.8 100.9 %all-to-all-start.2 = ((bf16[128,1,24,1280]{3,2,1,0:T(8,128)(2,1)}), bf16[128,1,24,1280]{3,2,1,0:T(8,128)(2,1)}, u32[]{:S(2)}, u32[]{:S(2)}) async-start(bf16[128,1,24,1280]{3,2,1,0:T(8,128)(2,1)} %bitcast.88), calls=%async_computation.2 | async-start | bytes 15728640 | tf_op jit(solution)/shard_map/all_to_all | solution.py:94
  339.8 4.4 %copy-start.3 = (f32[1,257,1280]{2,1,0:T(8,128)S(1)}, f32[1,257,1280]{2,1,0:T(8,128)}, u32[]{:S(2)}) copy-start(f32[1,257,1280]{2,1,0:T(8,128)} %copy-done.2) | copy-start | bytes 3947524
  344.2 3.0 copy-start.1
Sparse Core Ops, SparseCore 0:
  11.8 38.7 all-gather.1

commit v4 on v3

--- a/solution.py
+++ b/solution.py
@@ -36,31 +36,32 @@
     shard_rows = lax.all_gather(normed, "node", axis=0, tiled=True)
     number = shard_rows.shape[0]
     queries = jnp.einsum(
-        "ctd,de->cte", shard_rows, w_query, preferred_element_type=jnp.float32
+        "ctd,de->cet", shard_rows, w_query, preferred_element_type=jnp.float32
     ).astype(jnp.bfloat16)
     projected_keys = jnp.einsum(
-        "ctd,de->cte", shard_rows, w_key, preferred_element_type=jnp.float32
+        "ctd,de->cet", shard_rows, w_key, preferred_element_type=jnp.float32
     ).astype(jnp.bfloat16)
     projected_values = jnp.einsum(
-        "ctd,de->cte", shard_rows, w_value, preferred_element_type=jnp.float32
+        "ctd,de->cet", shard_rows, w_value, preferred_element_type=jnp.float32
     ).astype(jnp.bfloat16)
-    query_heads = queries.reshape(number, tokens_dev, local_heads, head_size)
-    key_heads = projected_keys.reshape(number, tokens_dev, local_heads, head_size)
-    value_heads = projected_values.reshape(number, tokens_dev, local_heads, head_size)
+    query_heads = queries.reshape(number, local_heads, head_size, tokens_dev)
+    key_heads = projected_keys.reshape(number, local_heads, head_size, tokens_dev)
+    value_heads = projected_values.reshape(number, local_heads, head_size, tokens_dev)
     scores = jnp.einsum(
-        "cqhd,ckhd->chqk", query_heads, key_heads, preferred_element_type=jnp.float32
+        "chdq,chdk->chqk", query_heads, key_heads, preferred_element_type=jnp.float32
     ) / math.sqrt(head_size)
     weights = jax.nn.softmax(scores, axis=-1).astype(jnp.bfloat16)
     mixture = jnp.einsum(
-        "chqk,ckhd->cqhd", weights, value_heads, preferred_element_type=jnp.float32
+        "chqk,chdk->cqhd", weights, value_heads, preferred_element_type=jnp.float32
     ).astype(jnp.bfloat16)
     head_results = mixture.reshape(number, tokens_dev, local_heads * head_size)
+    exchanged = lax.all_to_all(head_results, "node", split_axis=0, concat_axis=0, tiled=True)
     attention = jnp.einsum(
-        "itd,de->ite",
-        lax.all_to_all(head_results, "node", split_axis=0, concat_axis=2, tiled=True),
-        w_output,
+        "gtd,gde->te",
+        exchanged,
+        w_output.reshape(node_count, local_heads * head_size, width),
         preferred_element_type=jnp.float32,
-    )
+    ).reshape(local_images, tokens_dev, width)
     middle = inputs + attention
     normed_second = layer_norm(middle).astype(jnp.bfloat16)
     logits = jnp.einsum("itd,de->ite", normed_second, router, preferred_element_type=jnp.float32)

time: 359 us -> 354 us (0.986)
  local copies, waits for them, and re-layouts: 19.3 us -> 14.4 us
where the time goes in v4:
time: 354 us; the launch traced here: 349 us
  waiting for transfers between devices  135 us (38%)
  blocking collectives  101 us (29%)
  matrix products  58.7 us (17%)
  local copies, waits for them, and re-layouts  14.4 us (4%)
  other arithmetic  14.1 us (4%)
  between operations  13.6 us (4%)
  starting transfers between devices  12.6 us (4%)
    all_to_all x1, blocking collectives, shards(): lax.all_to_all(copies, ('node', 'ep'), split_axis=0, concat_axis=0, tiled...  101 us
    all_to_all x1, waiting for transfers between devices, shards(): lax.all_to_all(partial_sum, ('node', 'ep'), split_axis=0, concat_axis=0,...  92.2 us
    all_gather x1, waiting for transfers between devices, shards(): shard_rows = lax.all_gather(normed, 'node', axis=0, tiled=True)  32.3 us
    dot_general x1, matrix products, shards(): jnp.einsum('esf,efd->esd', hidden, w_out, preferred_element_type=jnp.floa...  25.7 us
    all_to_all x1, waiting for transfers between devices, shards(): lax.all_to_all(head_results, 'node', split_axis=0, concat_axis=0, tiled=T...  10.4 us
    all_to_all x1, starting transfers between devices, shards(): lax.all_to_all(partial_sum, ('node', 'ep'), split_axis=0, concat_axis=0,...  8.17 us
  transfers between devices with their start and end apart: 3, of which 3 were waited for; matrix products, arithmetic and copies ran while one was open for 2% of the time, Pallas kernels for 0%

profile of v4, /device:TPU:1, one launch (start us, length us, event | category | flops | bytes accessed | tf_op | source)
XLA Modules:
  0.0 349.2 jit_solution(14203628704890200238)
XLA Ops:
  6.5 1.4 convert_reduce_fusion
  8.0 1.4 fusion.32
  9.4 2.3 fusion.33
  12.0 0.6 copy_bitcast_fusion
  12.7 3.0 reduce-window.6
  16.0 0.8 broadcast.148
  16.8 1.6 reshape.285
  18.4 32.3 %all-gather.2.cloned.1.call-done = bf16[4,257,1280]{2,1,0:T(8,128)(2,1)} async-done(((bf16[1,257,1280]{2,1,0:T(8,128)(2,1)}), bf16[4,257,1280]{2,1,0:T(8,128)(2,1)}) %all-gather.2.cloned.1.call-update) | async-done | bytes 2631696 | tf_op jit(solution)/shard_map/all_gather | solution.py:36
  50.7 4.4 %fusion.36 = bf16[4,320,257]{1,2,0:T(8,128)(2,1)} fusion(bf16[4,257,1280]{2,1,0:T(8,128)(2,1)} %all-gather.2.cloned.1.call-done, bf16[1280,320]{0,1:T(8,128)(2,1)} %param.11), kind=kOutput, calls=%fused_computation.45 | convolution fusion | flops 842466560 | bytes 4108800 | tf_op jit(solution)/shard_map/ctd,de->cet/dot_general | solution.py:41
  55.1 2.3 copy.53
  57.4 4.4 %fusion.34 = bf16[4,320,257]{1,2,0:T(8,128)(2,1)} fusion(bf16[4,257,1280]{2,1,0:T(8,128)(2,1)} %all-gather.2.cloned.1.call-done, bf16[1280,320]{0,1:T(8,128)(2,1)} %param.12), kind=kOutput, calls=%fused_computation.43 | convolution fusion | flops 842466560 | bytes 4108800 | tf_op jit(solution)/shard_map/ctd,de->cet/dot_general | solution.py:44
  61.9 2.2 copy.51
  64.1 4.4 %fusion.35 = bf16[4,320,257]{1,2,0:T(8,128)(2,1)} fusion(bf16[4,257,1280]{2,1,0:T(8,128)(2,1)} %all-gather.2.cloned.1.call-done, bf16[1280,320]{0,1:T(8,128)(2,1)} %param.10), kind=kOutput, calls=%fused_computation.44 | convolution fusion | flops 842466560 | bytes 4108800 | tf_op jit(solution)/shard_map/ctd,de->cet/dot_general | solution.py:38
  68.5 2.3 copy.52
  70.8 6.5 %fusion.64 = (f32[4,4,257]{2,1,0:T(4,128)S(1)}, f32[4,4,257,257]{2,3,1,0:T(8,128)}) fusion(bf16[4,4,80,257]{3,2,1,0:T(8,128)(2,1)} %bitcast.100, bf16[4,4,80,257]{3,2,1,0:T(8,128)(2,1)} %bitcast.99), kind=kOutput, calls=%fused_computation.94 | convolution fusion | flops 172256048 | bytes 5559424 | tf_op jit(solution)/shard_map/sub | solution.py:53
  77.3 5.1 %fusion.31 = bf16[4,4,80,257]{3,2,1,0:T(8,128)(2,1)} fusion(bf16[4,4,80,257]{3,2,1,0:T(8,128)(2,1)} %bitcast.98, f32[4,4,257,257]{2,3,1,0:T(8,128)} %get-tuple-element.10, f32[4,4,257]{2,1,0:T(4,128)S(1)} %get-tuple-element.9), kind=kOutput, calls=%fused_computation.35 | convolution fusion | flops 171527968 | bytes 5559424 | tf_op jit(solution)/shard_map/chqk,chdk->cqhd/dot_general | solution.py:54
  82.5 2.2 copy.55
  84.7 4.4 %all-to-all-start = ((bf16[4,257,320]{2,1,0:T(8,128)(2,1)}), bf16[4,257,320]{2,1,0:T(8,128)(2,1)}, u32[]{:S(2)}, u32[]{:S(2)}) async-start(bf16[4,257,320]{2,1,0:T(8,128)(2,1)} %copy.55), calls=%async_computation | async-start | bytes 1622016 | tf_op jit(solution)/shard_map/all_to_all | solution.py:58
  89.1 0.9 fusion.57
  90.4 10.4 %all-to-all-done = bf16[4,257,320]{2,1,0:T(8,128)(2,1)} async-done(((bf16[4,257,320]{2,1,0:T(8,128)(2,1)}), bf16[4,257,320]{2,1,0:T(8,128)(2,1)}, u32[]{:S(2)}, u32[]{:S(2)}) %all-to-all-start) | async-done | bytes 657952 | tf_op jit(solution)/shard_map/all_to_all | solution.py:58
  100.8 3.6 %fusion.65 = (f32[257]{0:T(512)S(1)}, f32[1,257,1280]{2,1,0:T(8,128)S(1)}) fusion(bf16[4,257,320]{2,1,0:T(8,128)(2,1)} %all-to-all-done, bf16[4,320,1280]{2,1,0:T(8,128)(2,1)} %bitcast.103, bf16[1,257,1280]{2,1,0:T(8,128)(2,1)} %param.9), kind=kOutput, calls=%fused_computation.95 | convolution fusion | flops 843124224 | bytes 5909508 | tf_op jit(solution)/shard_map/gtd,gde->te/dot_general | solution.py:59
  104.3 0.3 multiply_reduce_fusion.1
  104.6 0.7 copy-done.2
  105.6 1.2 convolution_convert_fusion.1
  106.9 0.5 broadcast_in_dim.65
  107.4 101.0 %all_to_all.15 = bf16[128,1,24,1280]{3,2,1,0:T(8,128)(2,1)} all-to-all(bf16[128,1,24,1280]{3,2,1,0:T(8,128)(2,1)S(1)} %bitcast.92), channel_id=1, replica_groups=mesh['node'=4,'ep'=32] {'node','ep'}, dimensions={0} | all-to-all | bytes 15728640 | tf_op jit(solution)/shard_map/all_to_all | solution.py:86
  208.4 25.7 %convolution_convert_fusion = bf16[3072,1280]{1,0:T(8,128)(2,1)} fusion(bf16[1,1280,1280]{2,1,0:T(8,128)(2,1)S(1)} %copy-done, bf16[3072,1280]{1,0:T(8,128)(2,1)} %bitcast.94, bf16[1,1280,1280]{2,1,0:T(8,128)(2,1)} %param.15), kind=kOutput, calls=%fused_computation.10 | convolution fusion | flops 20171980800 | bytes 22282240 | tf_op jit(solution)/shard_map/esf,efd->esd/dot_general | solution.py:90
  234.1 8.2 %all-to-all-start.2 = ((bf16[128,1,24,1280]{3,2,1,0:T(8,128)(2,1)}), bf16[128,1,24,1280]{3,2,1,0:T(8,128)(2,1)}, u32[]{:S(2)}, u32[]{:S(2)}) async-start(bf16[128,1,24,1280]{3,2,1,0:T(8,128)(2,1)} %bitcast.93), calls=%async_computation.2 | async-start | bytes 15728640 | tf_op jit(solution)/shard_map/all_to_all | solution.py:95
  242.3 0.3 fusion.67
  242.8 92.2 %all-to-all-done.2 = bf16[128,1,24,1280]{3,2,1,0:T(8,128)(2,1)} async-done(((bf16[128,1,24,1280]{3,2,1,0:T(8,128)(2,1)}), bf16[128,1,24,1280]{3,2,1,0:T(8,128)(2,1)}, u32[]{:S(2)}, u32[]{:S(2)}) %all-to-all-start.2) | async-done | bytes 7864352 | tf_op jit(solution)/shard_map/all_to_all | solution.py:95
  335.0 4.4 %bitcast_reduce_fusion = bf16[32,24,1280]{2,1,0:T(8,128)(2,1)S(1)} fusion(bf16[4,32,24,1280]{3,2,1,0:T(8,128)(2,1)} %bitcast.91), kind=kLoop, calls=%fused_computation.11 | loop fusion | flops 2949120 | bytes 9830400 | tf_op jit(solution)/shard_map/reduce_sum | solution.py:99
  339.4 2.9 fusion.28
  (38 shorter events, 1.5 us)
Async XLA Ops:
  6.5 201.8 %copy-start = (bf16[1,1280,1280]{2,1,0:T(8,128)(2,1)S(1)}, bf16[1,1280,1280]{2,1,0:T(8,128)(2,1)}, u32[]{:S(2)}) copy-start(bf16[1,1280,1280]{2,1,0:T(8,128)(2,1)} %param.16) | copy-start | bytes 9830404
  6.5 5.2 %copy-start.7 = (s32[1,257,2]{1,2,0:T(2,128)S(1)}, s32[1,257,2]{1,2,0:T(2,128)}, u32[]{:S(2)}) copy-start(s32[1,257,2]{1,2,0:T(2,128)} %param.17) | copy-start | bytes 6172
  6.5 44.1 %all-gather.2.cloned.1.call-start = ((), (), s32[]{:S(2)}) async-start(), calls=%async_computation.3 | async-start | bytes 3379200 | tf_op jit(solution)/shard_map/all_gather | solution.py:36
  84.7 16.1 %all-to-all-start = ((bf16[4,257,320]{2,1,0:T(8,128)(2,1)}), bf16[4,257,320]{2,1,0:T(8,128)(2,1)}, u32[]{:S(2)}, u32[]{:S(2)}) async-start(bf16[4,257,320]{2,1,0:T(8,128)(2,1)} %copy.55), calls=%async_computation | async-start | bytes 1622016 | tf_op jit(solution)/shard_map/all_to_all | solution.py:58
  104.3 1.1 copy-start.2
  105.6 1.3 copy-start.4
  234.1 8.3 %copy-start.5 = (bf16[257,1280]{1,0:T(8,128)(2,1)S(1)}, bf16[257,1280]{1,0:T(8,128)(2,1)}, u32[]{:S(2)}) copy-start(bf16[257,1280]{1,0:T(8,128)(2,1)} %copy-done.4) | copy-start | bytes 1973764
  234.1 8.3 %copy-start.6 = (bf16[1280,32]{0,1:T(8,128)(2,1)S(1)}, bf16[1280,32]{0,1:T(8,128)(2,1)}, u32[]{:S(2)}) copy-start(bf16[1280,32]{0,1:T(8,128)(2,1)} %param.14) | copy-start | bytes 245764
  234.1 100.9 %all-to-all-start.2 = ((bf16[128,1,24,1280]{3,2,1,0:T(8,128)(2,1)}), bf16[128,1,24,1280]{3,2,1,0:T(8,128)(2,1)}, u32[]{:S(2)}, u32[]{:S(2)}) async-start(bf16[128,1,24,1280]{3,2,1,0:T(8,128)(2,1)} %bitcast.93), calls=%async_computation.2 | async-start | bytes 15728640 | tf_op jit(solution)/shard_map/all_to_all | solution.py:95
  335.0 4.4 %copy-start.3 = (f32[1,257,1280]{2,1,0:T(8,128)S(1)}, f32[1,257,1280]{2,1,0:T(8,128)}, u32[]{:S(2)}) copy-start(f32[1,257,1280]{2,1,0:T(8,128)} %copy-done.2) | copy-start | bytes 3947524
  339.4 3.0 copy-start.1
Sparse Core Ops, SparseCore 0:
  11.8 38.7 all-gather.1

commit v5 on v4

--- a/solution.py
+++ b/solution.py
@@ -33,7 +33,20 @@
     slot_count = local_images * CAP
     inputs = images.astype(jnp.float32)
     normed = layer_norm(inputs).astype(jnp.bfloat16)
-    shard_rows = lax.all_gather(normed, "node", axis=0, tiled=True)
+    node_index = lax.axis_index("node")
+    ahead = [(i, (i + 1) % node_count) for i in range(node_count)]
+    behind = [(i, (i - 1) % node_count) for i in range(node_count)]
+    split = width // 2
+    from_behind = lax.ppermute(normed, "node", ahead)
+    from_ahead = lax.ppermute(normed, "node", behind)
+    far = jnp.concatenate(
+        [
+            lax.ppermute(from_behind[..., :split], "node", ahead),
+            lax.ppermute(from_ahead[..., split:], "node", behind),
+        ],
+        axis=-1,
+    )
+    shard_rows = jnp.concatenate([normed, from_ahead, far, from_behind], axis=0)
     number = shard_rows.shape[0]
     queries = jnp.einsum(
         "ctd,de->cet", shard_rows, w_query, preferred_element_type=jnp.float32
@@ -54,7 +67,7 @@
     mixture = jnp.einsum(
         "chqk,chdk->cqhd", weights, value_heads, preferred_element_type=jnp.float32
     ).astype(jnp.bfloat16)
-    head_results = mixture.reshape(number, tokens_dev, local_heads * head_size)
+    head_results = jnp.roll(mixture.reshape(number, tokens_dev, local_heads * head_size), node_index, axis=0)
     exchanged = lax.all_to_all(head_results, "node", split_axis=0, concat_axis=0, tiled=True)
     attention = jnp.einsum(
         "gtd,gde->te",

time: 354 us -> 337 us (0.952)
  waiting for transfers between devices: 135 us -> 114 us
  between operations: 13.6 us -> 0.19 us
  starting transfers between devices: 12.6 us -> 18.8 us
  local copies, waits for them, and re-layouts: 14.4 us -> 18.5 us
  blocking collectives: 101 us -> 105 us
    all_gather x1 -> x0, waiting for transfers between devices: 32.3 us -> none  [shards(): shard_rows = lax.all_gather(normed, 'node', axis=0, tiled=True)]
    ppermute x0 -> x4, waiting for transfers between devices: none -> 13.2 us  [the longest x1 10.2 us: shards(): from_behind = lax.ppermute(normed, 'node', ahead)]
    ppermute x0 -> x4, starting transfers between devices: none -> 5.98 us  [the longest x1 2.39 us: shards(): lax.ppermute(from_ahead[..., split:], 'node', behind)]
    all_to_all x1, blocking collectives: 101 us -> 105 us  [shards(): lax.all_to_all(copies, ('node', 'ep'), split_axis=0, concat_axis=0, tiled...]
  transfers between devices with their start and end apart: 3 -> 6, of which waited for: 3 -> 5; matrix products, arithmetic and copies ran while one was open for 2% -> 4% of each run, Pallas kernels for 0% -> 0%
where the time goes in v5:
time: 337 us; the launch traced here: 331 us
  waiting for transfers between devices  114 us (34%)
  blocking collectives  105 us (31%)
  matrix products  58.7 us (17%)
  starting transfers between devices  18.8 us (6%)
  local copies, waits for them, and re-layouts  18.5 us (5%)
  other arithmetic  16.5 us (5%)
    all_to_all x1, blocking collectives, shards(): lax.all_to_all(copies, ('node', 'ep'), split_axis=0, concat_axis=0, tiled...  105 us
    all_to_all x1, waiting for transfers between devices, shards(): lax.all_to_all(partial_sum, ('node', 'ep'), split_axis=0, concat_axis=0,...  92.2 us
    dot_general x1, matrix products, shards(): jnp.einsum('esf,efd->esd', hidden, w_out, preferred_element_type=jnp.floa...  25.7 us
    ppermute x1, waiting for transfers between devices, shards(): from_behind = lax.ppermute(normed, 'node', ahead)  10.2 us
    all_to_all x1, waiting for transfers between devices, shards(): lax.all_to_all(head_results, 'node', split_axis=0, concat_axis=0, tiled=T...  8.18 us
    all_to_all x1, starting transfers between devices, shards(): lax.all_to_all(partial_sum, ('node', 'ep'), split_axis=0, concat_axis=0,...  8.17 us
  transfers between devices with their start and end apart: 6, of which 5 were waited for; matrix products, arithmetic and copies ran while one was open for 4% of the time, Pallas kernels for 0%

profile of v5, /device:TPU:1, one launch (start us, length us, event | category | flops | bytes accessed | tf_op | source)
XLA Modules:
  0.0 331.2 jit_solution(5253324336164317977)
XLA Ops:
  0.0 1.4 convert_reduce_fusion
  1.4 1.4 fusion.32
  2.9 2.3 fusion.33
  5.1 2.0 collective-permute-start.1
  7.2 1.3 collective-permute-start
  10.1 3.0 reduce-window.6
  13.1 10.2 %collective-permute-done.1 = bf16[1,257,1280]{2,1,0:T(8,128)(2,1)} collective-permute-done((bf16[1,257,1280]{2,1,0:T(8,128)(2,1)}, bf16[1,257,1280]{2,1,0:T(8,128)(2,1)}, u32[]{:S(2)}, u32[]{:S(2)}) %collective-permute-start.1) | collective-permute-done | bytes 657952 | tf_op jit(solution)/shard_map/ppermute | solution.py:40
  23.3 1.7 slice.38
  25.3 1.7 slice.39
  27.0 2.4 collective-permute-start.3
  30.5 1.6 reshape.285
  32.1 2.3 collective-permute-done.2
  35.1 4.4 %fusion.35 = bf16[4,320,257]{1,2,0:T(8,128)(2,1)} fusion(bf16[1280,320]{0,1:T(8,128)(2,1)} %param.10, bf16[1,257,1280]{2,1,0:T(8,128)(2,1)} %collective-permute-done.1, bf16[1,257,640]{2,1,0:T(8,128)(2,1)} %collective-permute-done.3, bf16[1,257,640]{2,1,0:T(8,128)(2,1)} %collective-permute-done.2, bf16[1,257,1280]{2,1,0:T(8,128)(2,1)} %collective-permute-done, ...), kind=kOutput, calls=%fused_computation.47 | convolution fusion | flops 855624960 | bytes 4108800 | tf_op jit(solution)/shard_map/ctd,de->cet/dot_general | solution.py:51
  39.6 2.3 copy.56
  41.8 4.4 %fusion.34 = bf16[4,320,257]{1,2,0:T(8,128)(2,1)} fusion(bf16[1280,320]{0,1:T(8,128)(2,1)} %param.12, bf16[1,257,1280]{2,1,0:T(8,128)(2,1)} %collective-permute-done.1, bf16[1,257,640]{2,1,0:T(8,128)(2,1)} %collective-permute-done.3, bf16[1,257,640]{2,1,0:T(8,128)(2,1)} %collective-permute-done.2, bf16[1,257,1280]{2,1,0:T(8,128)(2,1)} %collective-permute-done, ...), kind=kOutput, calls=%fused_computation.46 | convolution fusion | flops 855624960 | bytes 4108800 | tf_op jit(solution)/shard_map/ctd,de->cet/dot_general | solution.py:57
  46.3 2.2 copy.55
  48.5 4.4 %fusion.36 = bf16[4,320,257]{1,2,0:T(8,128)(2,1)} fusion(bf16[1280,320]{0,1:T(8,128)(2,1)} %param.11, bf16[1,257,1280]{2,1,0:T(8,128)(2,1)} %collective-permute-done.1, bf16[1,257,640]{2,1,0:T(8,128)(2,1)} %collective-permute-done.3, bf16[1,257,640]{2,1,0:T(8,128)(2,1)} %collective-permute-done.2, bf16[1,257,1280]{2,1,0:T(8,128)(2,1)} %collective-permute-done, ...), kind=kOutput, calls=%fused_computation.48 | convolution fusion | flops 855624960 | bytes 4108800 | tf_op jit(solution)/shard_map/ctd,de->cet/dot_general | solution.py:54
  53.0 2.3 copy.57
  55.3 6.5 %fusion.65 = (f32[4,4,257]{2,1,0:T(4,128)S(1)}, f32[4,4,257,257]{2,3,1,0:T(8,128)}) fusion(bf16[4,4,80,257]{3,2,1,0:T(8,128)(2,1)} %bitcast.96, bf16[4,4,80,257]{3,2,1,0:T(8,128)(2,1)} %bitcast.97), kind=kOutput, calls=%fused_computation.98 | convolution fusion | flops 172256048 | bytes 5559424 | tf_op jit(solution)/shard_map/sub | solution.py:66
  61.8 5.1 %fusion.31 = bf16[4,4,80,257]{3,2,1,0:T(8,128)(2,1)} fusion(bf16[4,4,80,257]{3,2,1,0:T(8,128)(2,1)} %bitcast.95, f32[4,4,257,257]{2,3,1,0:T(8,128)} %get-tuple-element.10, f32[4,4,257]{2,1,0:T(4,128)S(1)} %get-tuple-element.9), kind=kOutput, calls=%fused_computation.38 | convolution fusion | flops 171527968 | bytes 5559424 | tf_op jit(solution)/shard_map/chqk,chdk->cqhd/dot_general | solution.py:67
  66.9 2.2 copy.59
  69.1 2.4 fusion.42
  71.5 4.7 %all-to-all-start = ((bf16[4,257,320]{2,1,0:T(8,128)(2,1)}), bf16[4,257,320]{2,1,0:T(8,128)(2,1)}, u32[]{:S(2)}, u32[]{:S(2)}) async-start(bf16[4,257,320]{2,1,0:T(8,128)(2,1)} %fusion.42), calls=%async_computation | async-start | bytes 1622016 | tf_op jit(solution)/shard_map/all_to_all | solution.py:71
  77.5 8.2 %all-to-all-done = bf16[4,257,320]{2,1,0:T(8,128)(2,1)} async-done(((bf16[4,257,320]{2,1,0:T(8,128)(2,1)}), bf16[4,257,320]{2,1,0:T(8,128)(2,1)}, u32[]{:S(2)}, u32[]{:S(2)}) %all-to-all-start) | async-done | bytes 657952 | tf_op jit(solution)/shard_map/all_to_all | solution.py:71
  85.7 3.6 %fusion.66 = (f32[257]{0:T(512)S(1)}, f32[1,257,1280]{2,1,0:T(8,128)S(1)}) fusion(bf16[4,257,320]{2,1,0:T(8,128)(2,1)} %all-to-all-done, bf16[4,320,1280]{2,1,0:T(8,128)(2,1)} %bitcast.100, bf16[1,257,1280]{2,1,0:T(8,128)(2,1)} %param.9), kind=kOutput, calls=%fused_computation.99 | convolution fusion | flops 843124224 | bytes 5909508 | tf_op jit(solution)/shard_map/gtd,gde->te/dot_general | solution.py:72
  90.5 1.2 convolution_convert_fusion.1
  92.3 104.9 %all_to_all.15 = bf16[128,1,24,1280]{3,2,1,0:T(8,128)(2,1)} all-to-all(bf16[128,1,24,1280]{3,2,1,0:T(8,128)(2,1)S(1)} %bitcast.89), channel_id=1, replica_groups=mesh['node'=4,'ep'=32] {'node','ep'}, dimensions={0} | all-to-all | bytes 15728640 | tf_op jit(solution)/shard_map/all_to_all | solution.py:99
  197.2 25.7 %convolution_convert_fusion = bf16[3072,1280]{1,0:T(8,128)(2,1)} fusion(bf16[1,1280,1280]{2,1,0:T(8,128)(2,1)S(1)} %copy-done, bf16[3072,1280]{1,0:T(8,128)(2,1)} %bitcast.91, bf16[1,1280,1280]{2,1,0:T(8,128)(2,1)} %param.15), kind=kOutput, calls=%fused_computation.10 | convolution fusion | flops 20171980800 | bytes 22282240 | tf_op jit(solution)/shard_map/esf,efd->esd/dot_general | solution.py:103
  222.9 8.2 %all-to-all-start.2 = ((bf16[128,1,24,1280]{3,2,1,0:T(8,128)(2,1)}), bf16[128,1,24,1280]{3,2,1,0:T(8,128)(2,1)}, u32[]{:S(2)}, u32[]{:S(2)}) async-start(bf16[128,1,24,1280]{3,2,1,0:T(8,128)(2,1)} %bitcast.90), calls=%async_computation.2 | async-start | bytes 15728640 | tf_op jit(solution)/shard_map/all_to_all | solution.py:108
  231.6 92.2 %all-to-all-done.2 = bf16[128,1,24,1280]{3,2,1,0:T(8,128)(2,1)} async-done(((bf16[128,1,24,1280]{3,2,1,0:T(8,128)(2,1)}), bf16[128,1,24,1280]{3,2,1,0:T(8,128)(2,1)}, u32[]{:S(2)}, u32[]{:S(2)}) %all-to-all-start.2) | async-done | bytes 7864352 | tf_op jit(solution)/shard_map/all_to_all | solution.py:108
  323.8 4.4 %bitcast_reduce_fusion = bf16[32,24,1280]{2,1,0:T(8,128)(2,1)S(1)} fusion(bf16[4,32,24,1280]{3,2,1,0:T(8,128)(2,1)} %bitcast.88), kind=kLoop, calls=%fused_computation.11 | loop fusion | flops 2949120 | bytes 9830400 | tf_op jit(solution)/shard_map/reduce_sum | solution.py:112
  328.3 2.9 fusion.28
  (44 shorter events, 7.3 us)
Async XLA Ops:
  0.0 197.2 %copy-start = (bf16[1,1280,1280]{2,1,0:T(8,128)(2,1)S(1)}, bf16[1,1280,1280]{2,1,0:T(8,128)(2,1)}, u32[]{:S(2)}) copy-start(bf16[1,1280,1280]{2,1,0:T(8,128)(2,1)} %param.16) | copy-start | bytes 9830404
  5.1 18.1 %collective-permute-start.1 = (bf16[1,257,1280]{2,1,0:T(8,128)(2,1)}, bf16[1,257,1280]{2,1,0:T(8,128)(2,1)}, u32[]{:S(2)}, u32[]{:S(2)}) collective-permute-start(bf16[1,257,1280]{2,1,0:T(8,128)(2,1)} %fusion.33), channel_id=1, source_target_pairs={{0,32},{32,64},{64,96},{96,0},{1,33},{33,65},{65,97},{97,1},{2,34}... | collective-permute-start | bytes 1973768 | tf_op jit(solution)/shard_map/ppermute | solution.py:40
  7.2 18.1 %collective-permute-start = (bf16[1,257,1280]{2,1,0:T(8,128)(2,1)}, bf16[1,257,1280]{2,1,0:T(8,128)(2,1)}, u32[]{:S(2)}, u32[]{:S(2)}) collective-permute-start(bf16[1,257,1280]{2,1,0:T(8,128)(2,1)} %fusion.33), channel_id=1, source_target_pairs={{0,96},{32,0},{64,32},{96,64},{1,97},{33,1},{65,33},{97,65},{2,98}... | collective-permute-start | bytes 1973768 | tf_op jit(solution)/shard_map/ppermute | solution.py:41
  25.0 9.4 %collective-permute-start.2 = (bf16[1,257,640]{2,1,0:T(8,128)(2,1)}, bf16[1,257,640]{2,1,0:T(8,128)(2,1)}, u32[]{:S(2)}, u32[]{:S(2)}) collective-permute-start(bf16[1,257,640]{2,1,0:T(8,128)(2,1)} %slice.38), channel_id=1, source_target_pairs={{0,32},{32,64},{64,96},{96,0},{1,33},{33,65},{65,97},{97,1},{2,34}... | collective-permute-start | bytes 986888 | tf_op jit(solution)/shard_map/ppermute | solution.py:44
  27.0 8.1 %collective-permute-start.3 = (bf16[1,257,640]{2,1,0:T(8,128)(2,1)}, bf16[1,257,640]{2,1,0:T(8,128)(2,1)}, u32[]{:S(2)}, u32[]{:S(2)}) collective-permute-start(bf16[1,257,640]{2,1,0:T(8,128)(2,1)} %slice.39), channel_id=1, source_target_pairs={{0,96},{32,0},{64,32},{96,64},{1,97},{33,1},{65,33},{97,65},{2,98}... | collective-permute-start | bytes 986888 | tf_op jit(solution)/shard_map/ppermute | solution.py:45
  71.5 14.2 %all-to-all-start = ((bf16[4,257,320]{2,1,0:T(8,128)(2,1)}), bf16[4,257,320]{2,1,0:T(8,128)(2,1)}, u32[]{:S(2)}, u32[]{:S(2)}) async-start(bf16[4,257,320]{2,1,0:T(8,128)(2,1)} %fusion.42), calls=%async_computation | async-start | bytes 1622016 | tf_op jit(solution)/shard_map/all_to_all | solution.py:71
  89.2 1.1 copy-start.2
  90.5 1.3 copy-start.4
  222.9 8.3 %copy-start.5 = (bf16[257,1280]{1,0:T(8,128)(2,1)S(1)}, bf16[257,1280]{1,0:T(8,128)(2,1)}, u32[]{:S(2)}) copy-start(bf16[257,1280]{1,0:T(8,128)(2,1)} %copy-done.4) | copy-start | bytes 1973764
  222.9 8.3 %copy-start.6 = (bf16[1280,32]{0,1:T(8,128)(2,1)S(1)}, bf16[1280,32]{0,1:T(8,128)(2,1)}, u32[]{:S(2)}) copy-start(bf16[1280,32]{0,1:T(8,128)(2,1)} %param.14) | copy-start | bytes 245764
  222.9 100.9 %all-to-all-start.2 = ((bf16[128,1,24,1280]{3,2,1,0:T(8,128)(2,1)}), bf16[128,1,24,1280]{3,2,1,0:T(8,128)(2,1)}, u32[]{:S(2)}, u32[]{:S(2)}) async-start(bf16[128,1,24,1280]{3,2,1,0:T(8,128)(2,1)} %bitcast.90), calls=%async_computation.2 | async-start | bytes 15728640 | tf_op jit(solution)/shard_map/all_to_all | solution.py:108
  323.8 4.4 %copy-start.3 = (f32[1,257,1280]{2,1,0:T(8,128)S(1)}, f32[1,257,1280]{2,1,0:T(8,128)}, u32[]{:S(2)}) copy-start(f32[1,257,1280]{2,1,0:T(8,128)} %copy-done.2) | copy-start | bytes 3947524
  328.2 3.0 copy-start.1
